TPU v7x, 256 devices: a whole 4x4x8 slice. The times are simulated.
256 devices in a mesh: chan: 64 (over z, x, core), tm: 4 (over y).
Axes of the slice: x: 4, y: 4, z: 8, core: 2. Of those that a mesh axis runs over, the one named last changes fastest.
Arguments:
- voltages: bfloat16 [2, 2, 64, 2048, 2048], P(None, None, None, 'chan', 'tm'), may hold values from -6 to 6
- weights: bfloat16 [64, 2, 2, 32, 2048], P('chan'), may hold values from -0.09375 to 0.09375
- channel_map: int32 [64], replicated, may hold values from 0 to 63, each once
- sweep_response_taps: float32 [64, 2, 32, 256], P('chan', None, 'tm'), may hold values from -6 to 6
- chirp_length: int32 [32], P('tm'), may hold values from 32 to 256, as said below
Outputs:
- dedispersed: float32 [64, 2, 2, 32, 2048], P('chan', None, None, 'tm')
Inputs may be any that keep to these rules, and one draw needn't show every extreme that they name: `channel_map`: each channel appears once. `chirp_length`: one beam has the longest chirp of exactly 256 samples.
All inputs are finite; a program needn't handle non-finite values.
Results may differ from a plain program's by a relative error of at most 0.0003.
Values may be sent and summed in bfloat16 or wider, within the bound.
No kernel may reach another device: no remote copies, remote signals or barrier semaphores. Data moves between devices by JAX's collectives and lax.ppermute only.
A program may use at most 128 MiB of HBM per device.

v0:
```python
import math

import jax
import jax.numpy as jnp
from jax import lax
from jax.sharding import PartitionSpec as P


def mixing_matrix(weight_rows, axis):
    real_part = lax.index_in_dim(weight_rows, 0, axis, keepdims=False)
    imag_part = lax.index_in_dim(weight_rows, 1, axis, keepdims=False)
    upper = jnp.stack([real_part, -imag_part], axis=-2)
    lower = jnp.stack([imag_part, real_part], axis=-2)
    return jnp.stack([upper, lower], axis=axis)


def fourier_tables(extent):
    counter = jnp.arange(extent, dtype=jnp.int32)
    phase = counter[:, None] * counter[None, :] % extent
    angle = phase.astype(jnp.float32) * (2.0 * math.pi / extent)
    return lax.optimization_barrier((jnp.cos(angle), jnp.sin(angle)))


def product(left, right):
    return jnp.matmul(left, right, precision=lax.Precision.HIGH)


def build_dedispersion(sweep_response_taps, chirp_length):
    longest = sweep_response_taps.shape[3]
    block_size = 2 * longest
    cosines, sines = fourier_tables(block_size)
    lag = jnp.arange(longest, dtype=jnp.int32)
    inside = lag[None, :] < chirp_length[:, None]
    factor = lax.rsqrt(chirp_length.astype(jnp.float32))[:, None]
    resp_real = jnp.where(inside, sweep_response_taps[0, 0], 0.0) * factor
    resp_imag = jnp.where(inside, sweep_response_taps[0, 1], 0.0) * factor
    freq_real = product(resp_real, cosines[:longest]) + product(resp_imag, sines[:longest])
    freq_imag = product(resp_imag, cosines[:longest]) - product(resp_real, sines[:longest])
    gain_real = freq_real[:, None, :]
    gain_imag = freq_imag[:, None, :]
    back_cos = cosines[:, longest:]
    back_sin = sines[:, longest:]

    def dedisperse(series):
        total = series.shape[3]
        count = total // longest
        padding = jnp.zeros(series.shape[:3] + (longest,), jnp.float32)
        padded = jnp.concatenate([padding, series], axis=3)
        front = padded[..., :total].reshape(series.shape[:3] + (count, longest))
        behind = padded[..., longest:].reshape(series.shape[:3] + (count, longest))
        blocks = jnp.concatenate([front, behind], axis=4)
        spec_real = product(blocks[0], cosines) + product(blocks[1], sines)
        spec_imag = product(blocks[1], cosines) - product(blocks[0], sines)
        prod_real = spec_real * gain_real - spec_imag * gain_imag
        prod_imag = spec_real * gain_imag + spec_imag * gain_real
        out_real = (product(prod_real, back_cos) - product(prod_imag, back_sin)) / block_size
        out_imag = (product(prod_imag, back_cos) + product(prod_real, back_sin)) / block_size
        return jnp.stack([out_real, out_imag], 0).reshape(series.shape)

    return dedisperse


def ring_reduce_scatter(chunks, axis, size, split_axis):
    position = lax.axis_index(axis)
    halves = jnp.split(chunks, 2, axis=split_axis)
    forward = [(i, (i + 1) % size) for i in range(size)]
    backward = [(i, (i - 1) % size) for i in range(size)]

    def pick(part, index):
        return lax.dynamic_index_in_dim(part, index % size, 0, keepdims=False)

    acc_cw = pick(halves[0], position - 1)
    acc_ccw = pick(halves[1], position + 1)
    for step in range(size - 1):
        acc_cw = lax.ppermute(acc_cw, axis, forward) + pick(halves[0], position - step - 2)
        acc_ccw = lax.ppermute(acc_ccw, axis, backward) + pick(halves[1], position + step + 2)
    return jnp.concatenate([acc_cw, acc_ccw], axis=split_axis - 1)


def on_device(voltages, weights, channel_map, sweep_response_taps, chirp_length):
    zs, xs, cs = lax.axis_size("z"), lax.axis_size("x"), lax.axis_size("c")
    order = channel_map.reshape(zs, xs, cs).transpose(2, 0, 1)
    selected = jnp.moveaxis(jnp.take(voltages, order, axis=2, mode="clip"), 2, 0)
    own = lax.all_to_all(selected, "c", split_axis=0, concat_axis=5, tiled=True)[0]
    local_weights = lax.all_to_all(weights, ("z", "x"), split_axis=4, concat_axis=0, tiled=True)
    local_weights = local_weights.reshape((zs, xs) + local_weights.shape[1:])
    mixing = mixing_matrix(local_weights, 2)
    partial = jnp.einsum(
        "zxopbra,rpzxat->zxopbt",
        mixing,
        own,
        preferred_element_type=jnp.float32,
    )
    partial = ring_reduce_scatter(partial, "z", zs, 2)
    beams = ring_reduce_scatter(partial, "x", xs, 1)
    dedisperse = build_dedispersion(sweep_response_taps, chirp_length)
    result = dedisperse(lax.all_to_all(beams, "tm", split_axis=2, concat_axis=3, tiled=True))
    return result[None]


def solution(mesh):
    chan = mesh.shape["chan"]
    zs = 8 if chan % 8 == 0 and chan >= 16 else 1
    grid = mesh.devices.reshape(zs, chan // zs // 2, 2, mesh.shape["tm"])
    fine = jax.sharding.Mesh(grid, ("z", "x", "c", "tm"))
    antennas = ("z", "x", "c")
    return jax.shard_map(
        on_device,
        mesh=fine,
        in_specs=(
            P(None, None, None, antennas, "tm"),
            P(antennas, None, None, None, None),
            P(),
            P(antennas, None, "tm", None),
            P("tm"),
        ),
        out_specs=P(antennas, None, None, "tm", None),
        check_vma=False,
    )
```

profile of v0, /device:TPU:6, one launch (start us, length us, event | category | flops | bytes accessed | tf_op | source)
XLA Modules:
  0.0 215.8 jit_solution(1968922672968069277)
XLA Ops:
  1.0 9.0 %gather_fusion = bf16[64,2,2,32,512]{4,3,2,1,0:T(8,128)(2,1)} fusion(bf16[2,2,64,32,512]{4,3,2,1,0:T(8,128)(2,1)} %param.5, s32[1024]{0:T(1024)S(1)} %pad_clamp_fusion), kind=kCustom, calls=%fused_computation | custom fusion | bytes 16777472 | tf_op jit(solution)/shard_map/jit(_take)/gather | solution.py:83
  10.0 8.3 %copy.16 = bf16[64,2,2,32,512]{4,3,1,2,0:T(8,128)(2,1)} copy(bf16[64,2,2,32,512]{4,3,2,1,0:T(8,128)(2,1)} %gather_fusion) | data formatting | bytes 16777216 | tf_op jit(solution)/shard_map/jit(_take)/gather | solution.py:83
  18.3 7.1 %all-to-all-start = ((bf16[2,2,2,8,4,32,512]{6,5,1,2,4,3,0:T(8,128)(2,1)}), bf16[2,2,2,8,4,32,512]{6,5,1,2,4,3,0:T(8,128)(2,1)}, u32[]{:S(2)}, u32[]{:S(2)}) async-start(bf16[2,2,2,8,4,32,512]{6,5,1,2,4,3,0:T(8,128)(2,1)} %bitcast.151), calls=%async_computation | async-start | bytes 16777216 | tf_op jit(solution)/shard_map/all_to_all | solution.py:84
  29.6 3.3 %all-to-all-done = bf16[2,2,2,8,4,32,512]{6,5,1,2,4,3,0:T(8,128)(2,1)} async-done(((bf16[2,2,2,8,4,32,512]{6,5,1,2,4,3,0:T(8,128)(2,1)}), bf16[2,2,2,8,4,32,512]{6,5,1,2,4,3,0:T(8,128)(2,1)}, u32[]{:S(2)}, u32[]{:S(2)}) %all-to-all-start) | async-done | bytes 8388640 | tf_op jit(solution)/shard_map/all_to_all | solution.py:84
  32.9 11.6 %all-to-all-start.1 = ((bf16[32,2,4096]{2,1,0:T(2,128)(2,1)}), bf16[32,2,4096]{2,1,0:T(2,128)(2,1)S(1)}, u32[]{:S(2)}, u32[]{:S(2)}) async-start(bf16[32,2,4096]{2,1,0:T(2,128)(2,1)} %reshape.53), calls=%async_computation.1 | async-start | bytes 1048576 | tf_op jit(solution)/shard_map/all_to_all | solution.py:85
  44.4 8.3 %copy.17 = bf16[1,2,2,8,4,2,32,512]{7,6,5,1,2,4,3,0:T(8,128)(2,1)} copy(bf16[1,2,2,8,4,2,32,512]{7,6,1,2,4,3,5,0:T(8,128)(2,1)} %bitcast.4) | data formatting | bytes 16777216 | tf_op jit(solution)/shard_map/all_to_all | solution.py:84
  52.7 8.8 %all-to-all-done.1 = bf16[32,2,4096]{2,1,0:T(2,128)(2,1)S(1)} async-done(((bf16[32,2,4096]{2,1,0:T(2,128)(2,1)}), bf16[32,2,4096]{2,1,0:T(2,128)(2,1)S(1)}, u32[]{:S(2)}, u32[]{:S(2)}) %all-to-all-start.1) | async-done | bytes 524320 | tf_op jit(solution)/shard_map/all_to_all | solution.py:85
  65.9 8.1 %convolution_bitcast_fusion = f32[8,4,2,2,32,512]{5,4,2,3,1,0:T(8,128)} fusion(bf16[2,2,8,4,64,512,1]{5,4,0,6,1,3,2:T(8,128)(2,1)} %bitcast.150, bf16[8,4,1,2,32,2,64]{6,4,5,2,3,1,0:T(8,128)(2,1)S(1)} %get-tuple-element.22, bf16[8,4,1,2,32,2,64]{6,4,5,2,3,1,0:T(8,128)(2,1)S(1)} %get-tuple-element.21), kind=kOutput, calls=%fused_computation.1 | convolution fusion | flops 538968064 | bytes 17825792 | tf_op jit(solution)/shard_map/zxopbra,rpzxat->zxopbt/dot_general | solution.py:88
  74.0 6.9 %fusion.59 = (f32[8,4,1,2,32,512]{5,4,2,3,1,0:T(8,128)S(1)}, f32[8,4,1,2,32,512]{5,4,2,3,1,0:T(8,128)}) fusion(f32[8,4,2,2,32,512]{5,4,2,3,1,0:T(8,128)} %convolution_bitcast_fusion), kind=kLoop, calls=%fused_computation.117 | loop fusion | bytes 16777216 | tf_op jit(solution)/shard_map/split | solution.py:65
  87.4 9.3 %collective-permute-done = f32[4,1,2,32,512]{4,3,2,0,1:T(8,128)S(1)} collective-permute-done((f32[4,1,2,32,512]{4,3,2,0,1:T(8,128)S(1)}, f32[4,1,2,32,512]{4,3,2,0,1:T(8,128)S(1)}, u32[]{:S(2)}, u32[]{:S(2)}) %collective-permute-start) | collective-permute-done | bytes 524320 | tf_op jit(solution)/shard_map/ppermute | solution.py:75
  99.0 3.5 %collective-permute-start.11 = (f32[4,1,2,32,512]{4,3,2,0,1:T(8,128)S(1)}, f32[4,1,2,32,512]{4,3,2,0,1:T(8,128)S(1)}, u32[]{:S(2)}, u32[]{:S(2)}) collective-permute-start(f32[4,1,2,32,512]{4,3,2,0,1:T(8,128)S(1)} %bitcast_add_fusion.6), channel_id=1, source_target_pairs={{0,224},{32,0},{64,32},{96,64},{128,96},{160,128},{192,160},{224,1... | collective-permute-start | bytes 1572872 | tf_op jit(solution)/shard_map/ppermute | solution.py:76
  102.5 8.2 %collective-permute-done.1 = f32[4,1,2,32,512]{4,3,2,0,1:T(8,128)S(1)} collective-permute-done((f32[4,1,2,32,512]{4,3,2,0,1:T(8,128)S(1)}, f32[4,1,2,32,512]{4,3,2,0,1:T(8,128)S(1)}, u32[]{:S(2)}, u32[]{:S(2)}) %collective-permute-start.1) | collective-permute-done | bytes 524320 | tf_op jit(solution)/shard_map/ppermute | solution.py:75
  116.4 7.5 %collective-permute-done.2 = f32[4,1,2,32,512]{4,3,2,0,1:T(8,128)S(1)} collective-permute-done((f32[4,1,2,32,512]{4,3,2,0,1:T(8,128)S(1)}, f32[4,1,2,32,512]{4,3,2,0,1:T(8,128)S(1)}, u32[]{:S(2)}, u32[]{:S(2)}) %collective-permute-start.2) | collective-permute-done | bytes 524320 | tf_op jit(solution)/shard_map/ppermute | solution.py:75
  126.3 3.3 %collective-permute-start.13 = (f32[4,1,2,32,512]{4,3,2,0,1:T(8,128)S(1)}, f32[4,1,2,32,512]{4,3,2,0,1:T(8,128)S(1)}, u32[]{:S(2)}, u32[]{:S(2)}) collective-permute-start(f32[4,1,2,32,512]{4,3,2,0,1:T(8,128)S(1)} %bitcast_add_fusion.4), channel_id=1, source_target_pairs={{0,224},{32,0},{64,32},{96,64},{128,96},{160,128},{192,160},{224,1... | collective-permute-start | bytes 1572872 | tf_op jit(solution)/shard_map/ppermute | solution.py:76
  129.6 6.7 %collective-permute-done.3 = f32[4,1,2,32,512]{4,3,2,0,1:T(8,128)S(1)} collective-permute-done((f32[4,1,2,32,512]{4,3,2,0,1:T(8,128)S(1)}, f32[4,1,2,32,512]{4,3,2,0,1:T(8,128)S(1)}, u32[]{:S(2)}, u32[]{:S(2)}) %collective-permute-start.3) | collective-permute-done | bytes 524320 | tf_op jit(solution)/shard_map/ppermute | solution.py:75
  141.9 5.9 %collective-permute-done.4 = f32[4,1,2,32,512]{4,3,2,0,1:T(8,128)S(1)} collective-permute-done((f32[4,1,2,32,512]{4,3,2,0,1:T(8,128)S(1)}, f32[4,1,2,32,512]{4,3,2,0,1:T(8,128)S(1)}, u32[]{:S(2)}, u32[]{:S(2)}) %collective-permute-start.4) | collective-permute-done | bytes 524320 | tf_op jit(solution)/shard_map/ppermute | solution.py:75
  149.8 4.1 %fusion.23 = (f32[512,512]{1,0:T(8,128)S(1)}, f32[512,512]{1,0:T(8,128)S(1)}) fusion(), kind=kLoop, calls=%fused_computation.52 | loop fusion | flops 3670016 | bytes 2097152 | tf_op jit(solution)/shard_map/sin | solution.py:21
  155.0 3.3 %collective-permute-start.15 = (f32[4,1,2,32,512]{4,3,2,0,1:T(8,128)S(1)}, f32[4,1,2,32,512]{4,3,2,0,1:T(8,128)S(1)}, u32[]{:S(2)}, u32[]{:S(2)}) collective-permute-start(f32[4,1,2,32,512]{4,3,2,0,1:T(8,128)S(1)} %bitcast_add_fusion.2), channel_id=1, source_target_pairs={{0,224},{32,0},{64,32},{96,64},{128,96},{160,128},{192,160},{224,1... | collective-permute-start | bytes 1572872 | tf_op jit(solution)/shard_map/ppermute | solution.py:76
  163.8 3.6 %collective-permute-done.15 = f32[4,1,2,32,512]{4,3,2,0,1:T(8,128)S(1)} collective-permute-done((f32[4,1,2,32,512]{4,3,2,0,1:T(8,128)S(1)}, f32[4,1,2,32,512]{4,3,2,0,1:T(8,128)S(1)}, u32[]{:S(2)}, u32[]{:S(2)}) %collective-permute-start.15) | collective-permute-done | bytes 524320 | tf_op jit(solution)/shard_map/ppermute | solution.py:76
  168.5 3.8 %collective-permute-start.16 = (f32[4,1,2,32,512]{4,3,2,0,1:T(8,128)S(1)}, f32[4,1,2,32,512]{4,3,2,0,1:T(8,128)S(1)}, u32[]{:S(2)}, u32[]{:S(2)}) collective-permute-start(f32[4,1,2,32,512]{4,3,2,0,1:T(8,128)S(1)} %bitcast_add_fusion.1), channel_id=1, source_target_pairs={{0,224},{32,0},{64,32},{96,64},{128,96},{160,128},{192,160},{224,1... | collective-permute-start | bytes 1572872 | tf_op jit(solution)/shard_map/ppermute | solution.py:76
  187.0 3.3 %collective-permute-start.9 = (f32[1,2,32,512]{3,1,0,2:T(2,128)S(1)}, f32[1,2,32,512]{3,1,0,2:T(2,128)S(1)}, u32[]{:S(2)}, u32[]{:S(2)}) collective-permute-start(f32[1,2,32,512]{3,1,0,2:T(2,128)S(1)} %bitcast_add_fusion.18), channel_id=1, source_target_pairs={{0,8},{8,16},{16,24},{24,0},{1,9},{9,17},{17,25},{25,1},{2,10},{10... | collective-permute-start | bytes 393224 | tf_op jit(solution)/shard_map/ppermute | solution.py:75
  193.4 6.0 %collective-permute-done.19 = f32[1,2,32,512]{3,1,0,2:T(2,128)S(1)} collective-permute-done((f32[1,2,32,512]{3,1,0,2:T(2,128)S(1)}, f32[1,2,32,512]{3,1,0,2:T(2,128)S(1)}, u32[]{:S(2)}, u32[]{:S(2)}) %collective-permute-start.19) | collective-permute-done | bytes 131104 | tf_op jit(solution)/shard_map/ppermute | solution.py:76
  200.3 4.5 %all-to-all-start.2 = ((f32[2,2,32,512]{3,1,0,2:T(2,128)}), f32[2,2,32,512]{3,1,0,2:T(2,128)S(1)}, u32[]{:S(2)}, u32[]{:S(2)}) async-start(f32[2,2,32,512]{3,1,0,2:T(2,128)} %pad_maximum_fusion), calls=%async_computation.2 | async-start | bytes 524288 | tf_op jit(solution)/shard_map/all_to_all | solution.py:97
  205.1 6.4 %all-to-all-done.2 = f32[2,2,32,512]{3,1,0,2:T(2,128)S(1)} async-done(((f32[2,2,32,512]{3,1,0,2:T(2,128)}), f32[2,2,32,512]{3,1,0,2:T(2,128)S(1)}, u32[]{:S(2)}, u32[]{:S(2)}) %all-to-all-start.2) | async-done | bytes 262176 | tf_op jit(solution)/shard_map/all_to_all | solution.py:97
  (97 shorter events, 64.5 us)
Async XLA Ops:
  18.3 14.6 %all-to-all-start = ((bf16[2,2,2,8,4,32,512]{6,5,1,2,4,3,0:T(8,128)(2,1)}), bf16[2,2,2,8,4,32,512]{6,5,1,2,4,3,0:T(8,128)(2,1)}, u32[]{:S(2)}, u32[]{:S(2)}) async-start(bf16[2,2,2,8,4,32,512]{6,5,1,2,4,3,0:T(8,128)(2,1)} %bitcast.151), calls=%async_computation | async-start | bytes 16777216 | tf_op jit(solution)/shard_map/all_to_all | solution.py:84
  32.9 28.7 %all-to-all-start.1 = ((bf16[32,2,4096]{2,1,0:T(2,128)(2,1)}), bf16[32,2,4096]{2,1,0:T(2,128)(2,1)S(1)}, u32[]{:S(2)}, u32[]{:S(2)}) async-start(bf16[32,2,4096]{2,1,0:T(2,128)(2,1)} %reshape.53), calls=%async_computation.1 | async-start | bytes 1048576 | tf_op jit(solution)/shard_map/all_to_all | solution.py:85
  82.9 13.8 %collective-permute-start = (f32[4,1,2,32,512]{4,3,2,0,1:T(8,128)S(1)}, f32[4,1,2,32,512]{4,3,2,0,1:T(8,128)S(1)}, u32[]{:S(2)}, u32[]{:S(2)}) collective-permute-start(f32[4,1,2,32,512]{4,3,2,0,1:T(8,128)S(1)} %dynamic-slice_bitcast_fusion.1), channel_id=1, source_target_pairs={{0,32},{32,64},{64,96},{96,128},{128,160},{160,192},{192,224},{224... | collective-permute-start | bytes 1572872 | tf_op jit(solution)/shard_map/ppermute | solution.py:75
  84.7 13.2 %collective-permute-start.10 = (f32[4,1,2,32,512]{4,3,2,0,1:T(8,128)S(1)}, f32[4,1,2,32,512]{4,3,2,0,1:T(8,128)S(1)}, u32[]{:S(2)}, u32[]{:S(2)}) collective-permute-start(f32[4,1,2,32,512]{4,3,2,0,1:T(8,128)S(1)} %dynamic-slice_bitcast_fusion), channel_id=1, source_target_pairs={{0,224},{32,0},{64,32},{96,64},{128,96},{160,128},{192,160},{224,1... | collective-permute-start | bytes 1572872 | tf_op jit(solution)/shard_map/ppermute | solution.py:76
  97.8 12.9 %collective-permute-start.1 = (f32[4,1,2,32,512]{4,3,2,0,1:T(8,128)S(1)}, f32[4,1,2,32,512]{4,3,2,0,1:T(8,128)S(1)}, u32[]{:S(2)}, u32[]{:S(2)}) collective-permute-start(f32[4,1,2,32,512]{4,3,2,0,1:T(8,128)S(1)} %bitcast_add_fusion.13), channel_id=1, source_target_pairs={{0,32},{32,64},{64,96},{96,128},{128,160},{160,192},{192,224},{224... | collective-permute-start | bytes 1572872 | tf_op jit(solution)/shard_map/ppermute | solution.py:75
  99.0 12.9 %collective-permute-start.11 = (f32[4,1,2,32,512]{4,3,2,0,1:T(8,128)S(1)}, f32[4,1,2,32,512]{4,3,2,0,1:T(8,128)S(1)}, u32[]{:S(2)}, u32[]{:S(2)}) collective-permute-start(f32[4,1,2,32,512]{4,3,2,0,1:T(8,128)S(1)} %bitcast_add_fusion.6), channel_id=1, source_target_pairs={{0,224},{32,0},{64,32},{96,64},{128,96},{160,128},{192,160},{224,1... | collective-permute-start | bytes 1572872 | tf_op jit(solution)/shard_map/ppermute | solution.py:76
  111.8 30.0 %copy-start.3 = (s32[8]{0:T(128)S(1)}, s32[8]{0:T(128)}, u32[]{:S(2)}) copy-start(s32[8]{0:T(128)} %param.9) | copy-start | bytes 100
  111.9 12.1 %collective-permute-start.2 = (f32[4,1,2,32,512]{4,3,2,0,1:T(8,128)S(1)}, f32[4,1,2,32,512]{4,3,2,0,1:T(8,128)S(1)}, u32[]{:S(2)}, u32[]{:S(2)}) collective-permute-start(f32[4,1,2,32,512]{4,3,2,0,1:T(8,128)S(1)} %bitcast_add_fusion.12), channel_id=1, source_target_pairs={{0,32},{32,64},{64,96},{96,128},{128,160},{160,192},{192,224},{224... | collective-permute-start | bytes 1572872 | tf_op jit(solution)/shard_map/ppermute | solution.py:75
  113.1 12.0 %collective-permute-start.12 = (f32[4,1,2,32,512]{4,3,2,0,1:T(8,128)S(1)}, f32[4,1,2,32,512]{4,3,2,0,1:T(8,128)S(1)}, u32[]{:S(2)}, u32[]{:S(2)}) collective-permute-start(f32[4,1,2,32,512]{4,3,2,0,1:T(8,128)S(1)} %bitcast_add_fusion.5), channel_id=1, source_target_pairs={{0,224},{32,0},{64,32},{96,64},{128,96},{160,128},{192,160},{224,1... | collective-permute-start | bytes 1572872 | tf_op jit(solution)/shard_map/ppermute | solution.py:76
  125.0 11.2 %collective-permute-start.3 = (f32[4,1,2,32,512]{4,3,2,0,1:T(8,128)S(1)}, f32[4,1,2,32,512]{4,3,2,0,1:T(8,128)S(1)}, u32[]{:S(2)}, u32[]{:S(2)}) collective-permute-start(f32[4,1,2,32,512]{4,3,2,0,1:T(8,128)S(1)} %bitcast_add_fusion.11), channel_id=1, source_target_pairs={{0,32},{32,64},{64,96},{96,128},{128,160},{160,192},{192,224},{224... | collective-permute-start | bytes 1572872 | tf_op jit(solution)/shard_map/ppermute | solution.py:75
  126.3 11.2 %collective-permute-start.13 = (f32[4,1,2,32,512]{4,3,2,0,1:T(8,128)S(1)}, f32[4,1,2,32,512]{4,3,2,0,1:T(8,128)S(1)}, u32[]{:S(2)}, u32[]{:S(2)}) collective-permute-start(f32[4,1,2,32,512]{4,3,2,0,1:T(8,128)S(1)} %bitcast_add_fusion.4), channel_id=1, source_target_pairs={{0,224},{32,0},{64,32},{96,64},{128,96},{160,128},{192,160},{224,1... | collective-permute-start | bytes 1572872 | tf_op jit(solution)/shard_map/ppermute | solution.py:76
  137.4 10.5 %collective-permute-start.4 = (f32[4,1,2,32,512]{4,3,2,0,1:T(8,128)S(1)}, f32[4,1,2,32,512]{4,3,2,0,1:T(8,128)S(1)}, u32[]{:S(2)}, u32[]{:S(2)}) collective-permute-start(f32[4,1,2,32,512]{4,3,2,0,1:T(8,128)S(1)} %bitcast_add_fusion.10), channel_id=1, source_target_pairs={{0,32},{32,64},{64,96},{96,128},{128,160},{160,192},{192,224},{224... | collective-permute-start | bytes 1572872 | tf_op jit(solution)/shard_map/ppermute | solution.py:75
  138.6 15.3 %collective-permute-start.14 = (f32[4,1,2,32,512]{4,3,2,0,1:T(8,128)S(1)}, f32[4,1,2,32,512]{4,3,2,0,1:T(8,128)S(1)}, u32[]{:S(2)}, u32[]{:S(2)}) collective-permute-start(f32[4,1,2,32,512]{4,3,2,0,1:T(8,128)S(1)} %bitcast_add_fusion.3), channel_id=1, source_target_pairs={{0,224},{32,0},{64,32},{96,64},{128,96},{160,128},{192,160},{224,1... | collective-permute-start | bytes 1572872 | tf_op jit(solution)/shard_map/ppermute | solution.py:76
  149.8 11.6 %collective-permute-start.5 = (f32[4,1,2,32,512]{4,3,2,0,1:T(8,128)}, f32[4,1,2,32,512]{4,3,2,0,1:T(8,128)}, u32[]{:S(2)}, u32[]{:S(2)}) collective-permute-start(f32[4,1,2,32,512]{4,3,2,0,1:T(8,128)} %bitcast_add_fusion.9), channel_id=1, source_target_pairs={{0,32},{32,64},{64,96},{96,128},{128,160},{160,192},{192,224},{224... | collective-permute-start | bytes 1572872 | tf_op jit(solution)/shard_map/ppermute | solution.py:75
  155.0 12.3 %collective-permute-start.15 = (f32[4,1,2,32,512]{4,3,2,0,1:T(8,128)S(1)}, f32[4,1,2,32,512]{4,3,2,0,1:T(8,128)S(1)}, u32[]{:S(2)}, u32[]{:S(2)}) collective-permute-start(f32[4,1,2,32,512]{4,3,2,0,1:T(8,128)S(1)} %bitcast_add_fusion.2), channel_id=1, source_target_pairs={{0,224},{32,0},{64,32},{96,64},{128,96},{160,128},{192,160},{224,1... | collective-permute-start | bytes 1572872 | tf_op jit(solution)/shard_map/ppermute | solution.py:76
  163.4 10.7 %collective-permute-start.6 = (f32[4,1,2,32,512]{4,3,2,0,1:T(8,128)}, f32[4,1,2,32,512]{4,3,2,0,1:T(8,128)}, u32[]{:S(2)}, u32[]{:S(2)}) collective-permute-start(f32[4,1,2,32,512]{4,3,2,0,1:T(8,128)} %bitcast_add_fusion.8), channel_id=1, source_target_pairs={{0,32},{32,64},{64,96},{96,128},{128,160},{160,192},{192,224},{224... | collective-permute-start | bytes 1572872 | tf_op jit(solution)/shard_map/ppermute | solution.py:75
  168.5 10.5 %collective-permute-start.16 = (f32[4,1,2,32,512]{4,3,2,0,1:T(8,128)S(1)}, f32[4,1,2,32,512]{4,3,2,0,1:T(8,128)S(1)}, u32[]{:S(2)}, u32[]{:S(2)}) collective-permute-start(f32[4,1,2,32,512]{4,3,2,0,1:T(8,128)S(1)} %bitcast_add_fusion.1), channel_id=1, source_target_pairs={{0,224},{32,0},{64,32},{96,64},{128,96},{160,128},{192,160},{224,1... | collective-permute-start | bytes 1572872 | tf_op jit(solution)/shard_map/ppermute | solution.py:76
  175.6 5.5 %collective-permute-start.7 = (f32[1,2,32,512]{3,1,0,2:T(2,128)S(1)}, f32[1,2,32,512]{3,1,0,2:T(2,128)S(1)}, u32[]{:S(2)}, u32[]{:S(2)}) collective-permute-start(f32[1,2,32,512]{3,1,0,2:T(2,128)S(1)} %bitcast.160), channel_id=1, source_target_pairs={{0,8},{8,16},{16,24},{24,0},{1,9},{9,17},{17,25},{25,1},{2,10},{10... | collective-permute-start | bytes 393224 | tf_op jit(solution)/shard_map/ppermute | solution.py:75
  180.3 6.3 %collective-permute-start.17 = (f32[1,2,32,512]{3,1,0,2:T(2,128)S(1)}, f32[1,2,32,512]{3,1,0,2:T(2,128)S(1)}, u32[]{:S(2)}, u32[]{:S(2)}) collective-permute-start(f32[1,2,32,512]{3,1,0,2:T(2,128)S(1)} %bitcast.161), channel_id=1, source_target_pairs={{0,24},{8,0},{16,8},{24,16},{1,25},{9,1},{17,9},{25,17},{2,26},{10... | collective-permute-start | bytes 393224 | tf_op jit(solution)/shard_map/ppermute | solution.py:76
  181.2 5.6 %collective-permute-start.8 = (f32[1,2,32,512]{3,1,0,2:T(2,128)S(1)}, f32[1,2,32,512]{3,1,0,2:T(2,128)S(1)}, u32[]{:S(2)}, u32[]{:S(2)}) collective-permute-start(f32[1,2,32,512]{3,1,0,2:T(2,128)S(1)} %bitcast_add_fusion.19), channel_id=1, source_target_pairs={{0,8},{8,16},{16,24},{24,0},{1,9},{9,17},{17,25},{25,1},{2,10},{10... | collective-permute-start | bytes 393224 | tf_op jit(solution)/shard_map/ppermute | solution.py:75
  186.7 6.3 %collective-permute-start.18 = (f32[1,2,32,512]{3,1,0,2:T(2,128)S(1)}, f32[1,2,32,512]{3,1,0,2:T(2,128)S(1)}, u32[]{:S(2)}, u32[]{:S(2)}) collective-permute-start(f32[1,2,32,512]{3,1,0,2:T(2,128)S(1)} %bitcast_add_fusion.16), channel_id=1, source_target_pairs={{0,24},{8,0},{16,8},{24,16},{1,25},{9,1},{17,9},{25,17},{2,26},{10... | collective-permute-start | bytes 393224 | tf_op jit(solution)/shard_map/ppermute | solution.py:76
  187.0 6.2 %collective-permute-start.9 = (f32[1,2,32,512]{3,1,0,2:T(2,128)S(1)}, f32[1,2,32,512]{3,1,0,2:T(2,128)S(1)}, u32[]{:S(2)}, u32[]{:S(2)}) collective-permute-start(f32[1,2,32,512]{3,1,0,2:T(2,128)S(1)} %bitcast_add_fusion.18), channel_id=1, source_target_pairs={{0,8},{8,16},{16,24},{24,0},{1,9},{9,17},{17,25},{25,1},{2,10},{10... | collective-permute-start | bytes 393224 | tf_op jit(solution)/shard_map/ppermute | solution.py:75
  193.1 6.3 %collective-permute-start.19 = (f32[1,2,32,512]{3,1,0,2:T(2,128)S(1)}, f32[1,2,32,512]{3,1,0,2:T(2,128)S(1)}, u32[]{:S(2)}, u32[]{:S(2)}) collective-permute-start(f32[1,2,32,512]{3,1,0,2:T(2,128)S(1)} %bitcast_add_fusion.15), channel_id=1, source_target_pairs={{0,24},{8,0},{16,8},{24,16},{1,25},{9,1},{17,9},{25,17},{2,26},{10... | collective-permute-start | bytes 393224 | tf_op jit(solution)/shard_map/ppermute | solution.py:76
  200.3 11.1 %all-to-all-start.2 = ((f32[2,2,32,512]{3,1,0,2:T(2,128)}), f32[2,2,32,512]{3,1,0,2:T(2,128)S(1)}, u32[]{:S(2)}, u32[]{:S(2)}) async-start(f32[2,2,32,512]{3,1,0,2:T(2,128)} %pad_maximum_fusion), calls=%async_computation.2 | async-start | bytes 524288 | tf_op jit(solution)/shard_map/all_to_all | solution.py:97
  (3 other events, 37.9 us)
where the time goes:
time: 217 us; the launch traced here: 216 us
  waiting for transfers between devices  78.5 us (36%)
  starting transfers between devices  54.7 us (25%)
  local copies, waits for them, and re-layouts  45.4 us (21%)
  other arithmetic  24.6 us (11%)
  matrix products  11.9 us (5%)
    ppermute x10, waiting for transfers between devices, ring_reduce_scatter(): lax.ppermute(acc_cw, axis, forward) + pick(halves[0], position - step - 2)  42.1 us
    ppermute x10, starting transfers between devices, ring_reduce_scatter(): lax.ppermute(acc_ccw, axis, backward) + pick(halves[1], position + step + 2)  24 us
    ppermute x10, waiting for transfers between devices, ring_reduce_scatter(): lax.ppermute(acc_ccw, axis, backward) + pick(halves[1], position + step + 2)  17.8 us
    gather x2, local copies, waits for them, and re-layouts, on_device(): jnp.take(voltages, order, axis=2, mode='clip')  17.3 us
    all_to_all x1, starting transfers between devices, on_device(): lax.all_to_all(weights, ('z', 'x'), split_axis=4, concat_axis=0, tiled=True)  11.6 us
    add x10, other arithmetic, ring_reduce_scatter(): lax.ppermute(acc_cw, axis, forward) + pick(halves[0], position - step - 2)  10.2 us
    all_to_all x1, waiting for transfers between devices, on_device(): lax.all_to_all(weights, ('z', 'x'), split_axis=4, concat_axis=0, tiled=True)  8.82 us
    all_to_all x1, local copies, waits for them, and re-layouts, on_device(): lax.all_to_all(selected, 'c', split_axis=0, concat_axis=5, tiled=True)[0]  8.29 us
  transfers between devices with their start and end apart: 23, of which 15 were waited for; matrix products, arithmetic and copies ran while one was open for 17% of the time, Pallas kernels for 0%

commit v1 on v0

--- a/solution.py
+++ b/solution.py
@@ -62,18 +62,19 @@
 
 def ring_reduce_scatter(chunks, axis, size, split_axis):
     position = lax.axis_index(axis)
-    halves = jnp.split(chunks, 2, axis=split_axis)
+    half = chunks.shape[split_axis] // 2
     forward = [(i, (i + 1) % size) for i in range(size)]
     backward = [(i, (i - 1) % size) for i in range(size)]
 
-    def pick(part, index):
-        return lax.dynamic_index_in_dim(part, index % size, 0, keepdims=False)
+    def pick(which, index):
+        chunk = lax.dynamic_index_in_dim(chunks, index % size, 0, keepdims=False)
+        return lax.slice_in_dim(chunk, which * half, (which + 1) * half, axis=split_axis - 1)
 
-    acc_cw = pick(halves[0], position - 1)
-    acc_ccw = pick(halves[1], position + 1)
+    acc_cw = pick(0, position - 1)
+    acc_ccw = pick(1, position + 1)
     for step in range(size - 1):
-        acc_cw = lax.ppermute(acc_cw, axis, forward) + pick(halves[0], position - step - 2)
-        acc_ccw = lax.ppermute(acc_ccw, axis, backward) + pick(halves[1], position + step + 2)
+        acc_cw = lax.ppermute(acc_cw, axis, forward) + pick(0, position - step - 2)
+        acc_ccw = lax.ppermute(acc_ccw, axis, backward) + pick(1, position + step + 2)
     return jnp.concatenate([acc_cw, acc_ccw], axis=split_axis - 1)
 
 

time: 217 us -> 220 us (1.014)
  waiting for transfers between devices: 78.5 us -> 97 us
  other arithmetic: 24.6 us -> 9.13 us
    ppermute x20, waiting for transfers between devices: 59.9 us -> 78.7 us  [the longest x10 70.5 us: ring_reduce_scatter(): lax.ppermute(acc_ccw, axis, backward) + pick(1, position + step + 2)]
    add x20 -> x19, other arithmetic: 18.5 us -> 3.11 us  [the longest x10 2.48 us: ring_reduce_scatter(): acc_cw = lax.ppermute(acc_cw, axis, forward) + pick(0, position - step - 2)]
    split x1 -> x0, local copies, waits for them, and re-layouts: 6.92 us -> none  [ring_reduce_scatter(): halves = jnp.split(chunks, 2, axis=split_axis)]
    squeeze x2 -> x1, local copies, waits for them, and re-layouts: 1.12 us -> 7.63 us  [pick(): chunk = lax.dynamic_index_in_dim(chunks, index % size, 0, keepdims=False)]
    unnamed x13 -> x11, local copies, waits for them, and re-layouts: 7.29 us -> 5.33 us
  transfers between devices with their start and end apart: 23 -> 23, of which waited for: 15 -> 16; matrix products, arithmetic and copies ran while one was open for 17% -> 10% of each run, Pallas kernels for 0% -> 0%
where the time goes in v1:
time: 220 us; the launch traced here: 219 us
  waiting for transfers between devices  97 us (44%)
  starting transfers between devices  54.5 us (25%)
  local copies, waits for them, and re-layouts  43.9 us (20%)
  matrix products  14 us (6%)
  other arithmetic  9.13 us (4%)
    ppermute x10, waiting for transfers between devices, ring_reduce_scatter(): lax.ppermute(acc_ccw, axis, backward) + pick(1, position + step + 2)  70.5 us
    ppermute x10, starting transfers between devices, ring_reduce_scatter(): lax.ppermute(acc_ccw, axis, backward) + pick(1, position + step + 2)  19.5 us
    gather x2, local copies, waits for them, and re-layouts, on_device(): jnp.take(voltages, order, axis=2, mode='clip')  17.3 us
    ppermute x10, starting transfers between devices, ring_reduce_scatter(): acc_cw = lax.ppermute(acc_cw, axis, forward) + pick(0, position - step - 2)  11.9 us
    all_to_all x1, starting transfers between devices, on_device(): lax.all_to_all(weights, ('z', 'x'), split_axis=4, concat_axis=0, tiled=True)  11.6 us
    all_to_all x1, waiting for transfers between devices, on_device(): lax.all_to_all(weights, ('z', 'x'), split_axis=4, concat_axis=0, tiled=True)  8.59 us
    all_to_all x1, local copies, waits for them, and re-layouts, on_device(): lax.all_to_all(selected, 'c', split_axis=0, concat_axis=5, tiled=True)[0]  8.3 us
    ppermute x10, waiting for transfers between devices, ring_reduce_scatter(): acc_cw = lax.ppermute(acc_cw, axis, forward) + pick(0, position - step - 2)  8.15 us
  transfers between devices with their start and end apart: 23, of which 16 were waited for; matrix products, arithmetic and copies ran while one was open for 10% of the time, Pallas kernels for 0%

profile of v1, /device:TPU:6, one launch (start us, length us, event | category | flops | bytes accessed | tf_op | source)
XLA Modules:
  0.0 219.1 jit_solution(76331307453033760)
XLA Ops:
  1.0 9.0 %gather_fusion = bf16[64,2,2,32,512]{4,3,2,1,0:T(8,128)(2,1)} fusion(bf16[2,2,64,32,512]{4,3,2,1,0:T(8,128)(2,1)} %param.5, s32[1024]{0:T(1024)S(1)} %pad_clamp_fusion), kind=kCustom, calls=%fused_computation | custom fusion | bytes 16777472 | tf_op jit(solution)/shard_map/jit(_take)/gather | solution.py:84
  10.0 8.3 %copy.31 = bf16[64,2,2,32,512]{4,3,1,2,0:T(8,128)(2,1)} copy(bf16[64,2,2,32,512]{4,3,2,1,0:T(8,128)(2,1)} %gather_fusion) | data formatting | bytes 16777216 | tf_op jit(solution)/shard_map/jit(_take)/gather | solution.py:84
  18.3 7.1 %all-to-all-start = ((bf16[2,2,2,8,4,32,512]{6,5,1,2,4,3,0:T(8,128)(2,1)}), bf16[2,2,2,8,4,32,512]{6,5,1,2,4,3,0:T(8,128)(2,1)}, u32[]{:S(2)}, u32[]{:S(2)}) async-start(bf16[2,2,2,8,4,32,512]{6,5,1,2,4,3,0:T(8,128)(2,1)} %bitcast.202), calls=%async_computation | async-start | bytes 16777216 | tf_op jit(solution)/shard_map/all_to_all | solution.py:85
  32.9 11.6 %all-to-all-start.1 = ((bf16[32,2,4096]{2,1,0:T(2,128)(2,1)}), bf16[32,2,4096]{2,1,0:T(2,128)(2,1)S(1)}, u32[]{:S(2)}, u32[]{:S(2)}) async-start(bf16[32,2,4096]{2,1,0:T(2,128)(2,1)} %reshape.61), calls=%async_computation.1 | async-start | bytes 1048576 | tf_op jit(solution)/shard_map/all_to_all | solution.py:86
  44.7 8.3 %copy.32 = bf16[1,2,2,8,4,2,32,512]{7,6,5,1,2,4,3,0:T(8,128)(2,1)} copy(bf16[1,2,2,8,4,2,32,512]{7,6,1,2,4,3,5,0:T(8,128)(2,1)} %bitcast.4) | data formatting | bytes 16777216 | tf_op jit(solution)/shard_map/all_to_all | solution.py:85
  53.0 8.6 %all-to-all-done.1 = bf16[32,2,4096]{2,1,0:T(2,128)(2,1)S(1)} async-done(((bf16[32,2,4096]{2,1,0:T(2,128)(2,1)}), bf16[32,2,4096]{2,1,0:T(2,128)(2,1)S(1)}, u32[]{:S(2)}, u32[]{:S(2)}) %all-to-all-start.1) | async-done | bytes 524320 | tf_op jit(solution)/shard_map/all_to_all | solution.py:86
  65.9 8.1 %convolution_bitcast_fusion = f32[8,4,2,512,2,32]{3,5,4,2,1,0:T(8,128)} fusion(bf16[2,2,8,4,64,512,1]{5,4,0,6,1,3,2:T(8,128)(2,1)} %bitcast.201, bf16[8,4,1,2,32,2,64]{6,4,5,2,3,1,0:T(8,128)(2,1)S(1)} %get-tuple-element.32, bf16[8,4,1,2,32,2,64]{6,4,5,2,3,1,0:T(8,128)(2,1)S(1)} %get-tuple-element.31), kind=kOutput, calls=%fused_computation.1 | convolution fusion | flops 538968064 | bytes 17825792 | tf_op jit(solution)/shard_map/zxopbra,rpzxat->zxopbt/dot_general | solution.py:89
  74.0 7.6 %dynamic-slice_bitcast_fusion = (f32[4,2,2,32,512]{4,3,1,2,0:T(8,128)S(1)}, f32[4,2,2,32,512]{4,3,1,2,0:T(8,128)S(1)}, f32[4,2,2,32,512]{4,3,1,2,0:T(8,128)S(1)}...) fusion(f32[8,4,2,512,2,32]{3,5,4,2,1,0:T(8,128)} %convolution_b, ...), kind=kLoop, calls=%fused_computation.45 | loop fusion | bytes 33554496 | tf_op jit(solution)/shard_map/jit(dynamic_index_in_dim)/squeeze | solution.py:70
  83.9 10.3 %collective-permute-done.7 = f32[4,1,2,32,512]{4,3,1,2,0:T(8,128)S(1)} collective-permute-done((f32[4,1,2,32,512]{4,3,1,2,0:T(8,128)S(1)}, f32[4,1,2,32,512]{4,3,1,2,0:T(8,128)S(1)}, u32[]{:S(2)}, u32[]{:S(2)}) %collective-permute-start.7) | collective-permute-done | bytes 524320 | tf_op jit(solution)/shard_map/ppermute | solution.py:77
  96.8 9.3 %collective-permute-done.8 = f32[4,1,2,32,512]{4,3,1,2,0:T(8,128)S(1)} collective-permute-done((f32[4,1,2,32,512]{4,3,1,2,0:T(8,128)S(1)}, f32[4,1,2,32,512]{4,3,1,2,0:T(8,128)S(1)}, u32[]{:S(2)}, u32[]{:S(2)}) %collective-permute-start.8) | collective-permute-done | bytes 524320 | tf_op jit(solution)/shard_map/ppermute | solution.py:77
  109.3 8.7 %collective-permute-done.9 = f32[4,1,2,32,512]{4,3,1,2,0:T(8,128)S(1)} collective-permute-done((f32[4,1,2,32,512]{4,3,1,2,0:T(8,128)S(1)}, f32[4,1,2,32,512]{4,3,1,2,0:T(8,128)S(1)}, u32[]{:S(2)}, u32[]{:S(2)}) %collective-permute-start.9) | collective-permute-done | bytes 524320 | tf_op jit(solution)/shard_map/ppermute | solution.py:77
  121.7 8.1 %collective-permute-done.10 = f32[4,1,2,32,512]{4,3,1,2,0:T(8,128)S(1)} collective-permute-done((f32[4,1,2,32,512]{4,3,1,2,0:T(8,128)S(1)}, f32[4,1,2,32,512]{4,3,1,2,0:T(8,128)S(1)}, u32[]{:S(2)}, u32[]{:S(2)}) %collective-permute-start.10) | collective-permute-done | bytes 524320 | tf_op jit(solution)/shard_map/ppermute | solution.py:77
  130.0 3.7 %collective-permute-start.11 = (f32[4,1,2,32,512]{4,3,1,2,0:T(8,128)S(1)}, f32[4,1,2,32,512]{4,3,1,2,0:T(8,128)S(1)}, u32[]{:S(2)}, u32[]{:S(2)}) collective-permute-start(f32[4,1,2,32,512]{4,3,1,2,0:T(8,128)S(1)} %slice_add_fusion.3), channel_id=1, source_target_pairs={{0,224},{32,0},{64,32},{96,64},{128,96},{160,128},{192,160},{224,1... | collective-permute-start | bytes 1572872 | tf_op jit(solution)/shard_map/ppermute | solution.py:77
  133.8 8.1 %collective-permute-done.11 = f32[4,1,2,32,512]{4,3,1,2,0:T(8,128)S(1)} collective-permute-done((f32[4,1,2,32,512]{4,3,1,2,0:T(8,128)S(1)}, f32[4,1,2,32,512]{4,3,1,2,0:T(8,128)S(1)}, u32[]{:S(2)}, u32[]{:S(2)}) %collective-permute-start.11) | collective-permute-done | bytes 524320 | tf_op jit(solution)/shard_map/ppermute | solution.py:77
  145.9 9.0 %collective-permute-done.12 = f32[4,1,2,32,512]{4,3,1,2,0:T(8,128)S(1)} collective-permute-done((f32[4,1,2,32,512]{4,3,1,2,0:T(8,128)S(1)}, f32[4,1,2,32,512]{4,3,1,2,0:T(8,128)S(1)}, u32[]{:S(2)}, u32[]{:S(2)}) %collective-permute-start.12) | collective-permute-done | bytes 524320 | tf_op jit(solution)/shard_map/ppermute | solution.py:77
  155.1 3.8 %collective-permute-start.13 = (f32[4,1,2,32,512]{4,3,1,2,0:T(8,128)S(1)}, f32[4,1,2,32,512]{4,3,1,2,0:T(8,128)S(1)}, u32[]{:S(2)}, u32[]{:S(2)}) collective-permute-start(f32[4,1,2,32,512]{4,3,1,2,0:T(8,128)S(1)} %slice_add_fusion.1), channel_id=1, source_target_pairs={{0,224},{32,0},{64,32},{96,64},{128,96},{160,128},{192,160},{224,1... | collective-permute-start | bytes 1572872 | tf_op jit(solution)/shard_map/ppermute | solution.py:77
  159.7 5.8 %collective-permute-done.13 = f32[4,1,2,32,512]{4,3,1,2,0:T(8,128)S(1)} collective-permute-done((f32[4,1,2,32,512]{4,3,1,2,0:T(8,128)S(1)}, f32[4,1,2,32,512]{4,3,1,2,0:T(8,128)S(1)}, u32[]{:S(2)}, u32[]{:S(2)}) %collective-permute-start.13) | collective-permute-done | bytes 524320 | tf_op jit(solution)/shard_map/ppermute | solution.py:77
  165.6 4.8 %collective-permute-done.6 = f32[4,1,2,32,512]{4,3,1,2,0:T(8,128)} collective-permute-done((f32[4,1,2,32,512]{4,3,1,2,0:T(8,128)}, f32[4,1,2,32,512]{4,3,1,2,0:T(8,128)}, u32[]{:S(2)}, u32[]{:S(2)}) %collective-permute-start.6) | collective-permute-done | bytes 524320 | tf_op jit(solution)/shard_map/ppermute | solution.py:76
  173.5 4.1 %fusion.23 = (f32[512,512]{1,0:T(8,128)S(1)}, f32[512,512]{1,0:T(8,128)S(1)}) fusion(), kind=kLoop, calls=%fused_computation.84 | loop fusion | flops 3670016 | bytes 2097152 | tf_op jit(solution)/shard_map/sin | solution.py:21
  183.3 3.7 %collective-permute-start.16 = (f32[1,2,32,512]{3,2,1,0:T(8,128)S(1)}, f32[1,2,32,512]{3,2,1,0:T(8,128)S(1)}, u32[]{:S(2)}, u32[]{:S(2)}) collective-permute-start(f32[1,2,32,512]{3,2,1,0:T(8,128)S(1)} %fusion.53), channel_id=1, source_target_pairs={{0,8},{8,16},{16,24},{24,0},{1,9},{9,17},{17,25},{25,1},{2,10},{10... | collective-permute-start | bytes 393224 | tf_op jit(solution)/shard_map/ppermute | solution.py:76
  190.6 5.7 %collective-permute-done.18 = f32[1,2,32,512]{3,2,1,0:T(8,128)S(1)} collective-permute-done((f32[1,2,32,512]{3,2,1,0:T(8,128)S(1)}, f32[1,2,32,512]{3,2,1,0:T(8,128)S(1)}, u32[]{:S(2)}, u32[]{:S(2)}) %collective-permute-start.18) | collective-permute-done | bytes 131104 | tf_op jit(solution)/shard_map/ppermute | solution.py:77
  197.3 5.3 %collective-permute-done.19 = f32[1,2,32,512]{3,2,1,0:T(8,128)S(1)} collective-permute-done((f32[1,2,32,512]{3,2,1,0:T(8,128)S(1)}, f32[1,2,32,512]{3,2,1,0:T(8,128)S(1)}, u32[]{:S(2)}, u32[]{:S(2)}) %collective-permute-start.19) | collective-permute-done | bytes 131104 | tf_op jit(solution)/shard_map/ppermute | solution.py:77
  203.5 4.5 %all-to-all-start.2 = ((f32[2,2,32,512]{3,1,0,2:T(2,128)}), f32[2,2,32,512]{3,1,0,2:T(2,128)S(1)}, u32[]{:S(2)}, u32[]{:S(2)}) async-start(f32[2,2,32,512]{3,1,0,2:T(2,128)} %copy.43), calls=%async_computation.2 | async-start | bytes 524288 | tf_op jit(solution)/shard_map/all_to_all | solution.py:98
  208.2 6.4 %all-to-all-done.2 = f32[2,2,32,512]{3,1,0,2:T(2,128)S(1)} async-done(((f32[2,2,32,512]{3,1,0,2:T(2,128)}), f32[2,2,32,512]{3,1,0,2:T(2,128)S(1)}, u32[]{:S(2)}, u32[]{:S(2)}) %all-to-all-start.2) | async-done | bytes 262176 | tf_op jit(solution)/shard_map/all_to_all | solution.py:98
  (92 shorter events, 48.5 us)
Async XLA Ops:
  18.3 14.6 %all-to-all-start = ((bf16[2,2,2,8,4,32,512]{6,5,1,2,4,3,0:T(8,128)(2,1)}), bf16[2,2,2,8,4,32,512]{6,5,1,2,4,3,0:T(8,128)(2,1)}, u32[]{:S(2)}, u32[]{:S(2)}) async-start(bf16[2,2,2,8,4,32,512]{6,5,1,2,4,3,0:T(8,128)(2,1)} %bitcast.202), calls=%async_computation | async-start | bytes 16777216 | tf_op jit(solution)/shard_map/all_to_all | solution.py:85
  32.9 28.7 %all-to-all-start.1 = ((bf16[32,2,4096]{2,1,0:T(2,128)(2,1)}), bf16[32,2,4096]{2,1,0:T(2,128)(2,1)S(1)}, u32[]{:S(2)}, u32[]{:S(2)}) async-start(bf16[32,2,4096]{2,1,0:T(2,128)(2,1)} %reshape.61), calls=%async_computation.1 | async-start | bytes 1048576 | tf_op jit(solution)/shard_map/all_to_all | solution.py:86
  81.7 12.6 %collective-permute-start.7 = (f32[4,1,2,32,512]{4,3,1,2,0:T(8,128)S(1)}, f32[4,1,2,32,512]{4,3,1,2,0:T(8,128)S(1)}, u32[]{:S(2)}, u32[]{:S(2)}) collective-permute-start(f32[4,1,2,32,512]{4,3,1,2,0:T(8,128)S(1)} %slice.188), channel_id=1, source_target_pairs={{0,224},{32,0},{64,32},{96,64},{128,96},{160,128},{192,160},{224,1... | collective-permute-start | bytes 1572872 | tf_op jit(solution)/shard_map/ppermute | solution.py:77
  81.8 14.1 %collective-permute-start = (f32[4,1,2,32,512]{4,3,1,2,0:T(8,128)S(1)}, f32[4,1,2,32,512]{4,3,1,2,0:T(8,128)S(1)}, u32[]{:S(2)}, u32[]{:S(2)}) collective-permute-start(f32[4,1,2,32,512]{4,3,1,2,0:T(8,128)S(1)} %slice.180), channel_id=1, source_target_pairs={{0,32},{32,64},{64,96},{96,128},{128,160},{160,192},{192,224},{224... | collective-permute-start | bytes 1572872 | tf_op jit(solution)/shard_map/ppermute | solution.py:76
  94.3 11.7 %collective-permute-start.8 = (f32[4,1,2,32,512]{4,3,1,2,0:T(8,128)S(1)}, f32[4,1,2,32,512]{4,3,1,2,0:T(8,128)S(1)}, u32[]{:S(2)}, u32[]{:S(2)}) collective-permute-start(f32[4,1,2,32,512]{4,3,1,2,0:T(8,128)S(1)} %slice_add_fusion.6), channel_id=1, source_target_pairs={{0,224},{32,0},{64,32},{96,64},{128,96},{160,128},{192,160},{224,1... | collective-permute-start | bytes 1572872 | tf_op jit(solution)/shard_map/ppermute | solution.py:77
  96.0 13.2 %collective-permute-start.1 = (f32[4,1,2,32,512]{4,3,1,2,0:T(8,128)S(1)}, f32[4,1,2,32,512]{4,3,1,2,0:T(8,128)S(1)}, u32[]{:S(2)}, u32[]{:S(2)}) collective-permute-start(f32[4,1,2,32,512]{4,3,1,2,0:T(8,128)S(1)} %slice_add_fusion.13), channel_id=1, source_target_pairs={{0,32},{32,64},{64,96},{96,128},{128,160},{160,192},{192,224},{224... | collective-permute-start | bytes 1572872 | tf_op jit(solution)/shard_map/ppermute | solution.py:76
  106.1 12.0 %collective-permute-start.9 = (f32[4,1,2,32,512]{4,3,1,2,0:T(8,128)S(1)}, f32[4,1,2,32,512]{4,3,1,2,0:T(8,128)S(1)}, u32[]{:S(2)}, u32[]{:S(2)}) collective-permute-start(f32[4,1,2,32,512]{4,3,1,2,0:T(8,128)S(1)} %slice_add_fusion.5), channel_id=1, source_target_pairs={{0,224},{32,0},{64,32},{96,64},{128,96},{160,128},{192,160},{224,1... | collective-permute-start | bytes 1572872 | tf_op jit(solution)/shard_map/ppermute | solution.py:77
  109.2 12.3 %collective-permute-start.2 = (f32[4,1,2,32,512]{4,3,1,2,0:T(8,128)S(1)}, f32[4,1,2,32,512]{4,3,1,2,0:T(8,128)S(1)}, u32[]{:S(2)}, u32[]{:S(2)}) collective-permute-start(f32[4,1,2,32,512]{4,3,1,2,0:T(8,128)S(1)} %slice_add_fusion.12), channel_id=1, source_target_pairs={{0,32},{32,64},{64,96},{96,128},{128,160},{160,192},{192,224},{224... | collective-permute-start | bytes 1572872 | tf_op jit(solution)/shard_map/ppermute | solution.py:76
  118.2 11.7 %collective-permute-start.10 = (f32[4,1,2,32,512]{4,3,1,2,0:T(8,128)S(1)}, f32[4,1,2,32,512]{4,3,1,2,0:T(8,128)S(1)}, u32[]{:S(2)}, u32[]{:S(2)}) collective-permute-start(f32[4,1,2,32,512]{4,3,1,2,0:T(8,128)S(1)} %slice_add_fusion.4), channel_id=1, source_target_pairs={{0,224},{32,0},{64,32},{96,64},{128,96},{160,128},{192,160},{224,1... | collective-permute-start | bytes 1572872 | tf_op jit(solution)/shard_map/ppermute | solution.py:77
  121.7 12.0 %collective-permute-start.3 = (f32[4,1,2,32,512]{4,3,1,2,0:T(8,128)S(1)}, f32[4,1,2,32,512]{4,3,1,2,0:T(8,128)S(1)}, u32[]{:S(2)}, u32[]{:S(2)}) collective-permute-start(f32[4,1,2,32,512]{4,3,1,2,0:T(8,128)S(1)} %slice_add_fusion.11), channel_id=1, source_target_pairs={{0,32},{32,64},{64,96},{96,128},{128,160},{160,192},{192,224},{224... | collective-permute-start | bytes 1572872 | tf_op jit(solution)/shard_map/ppermute | solution.py:76
  130.0 12.0 %collective-permute-start.11 = (f32[4,1,2,32,512]{4,3,1,2,0:T(8,128)S(1)}, f32[4,1,2,32,512]{4,3,1,2,0:T(8,128)S(1)}, u32[]{:S(2)}, u32[]{:S(2)}) collective-permute-start(f32[4,1,2,32,512]{4,3,1,2,0:T(8,128)S(1)} %slice_add_fusion.3), channel_id=1, source_target_pairs={{0,224},{32,0},{64,32},{96,64},{128,96},{160,128},{192,160},{224,1... | collective-permute-start | bytes 1572872 | tf_op jit(solution)/shard_map/ppermute | solution.py:77
  133.7 53.3 %copy-start.1 = (f32[1,2,8,256]{3,2,1,0:T(8,128)S(1)}, f32[1,2,8,256]{3,2,1,0:T(8,128)}, u32[]{:S(2)}) copy-start(f32[1,2,8,256]{3,2,1,0:T(8,128)} %param.8) | copy-start | bytes 49156
  133.7 12.0 %collective-permute-start.4 = (f32[4,1,2,32,512]{4,3,1,2,0:T(8,128)S(1)}, f32[4,1,2,32,512]{4,3,1,2,0:T(8,128)S(1)}, u32[]{:S(2)}, u32[]{:S(2)}) collective-permute-start(f32[4,1,2,32,512]{4,3,1,2,0:T(8,128)S(1)} %slice_add_fusion.10), channel_id=1, source_target_pairs={{0,32},{32,64},{64,96},{96,128},{128,160},{160,192},{192,224},{224... | collective-permute-start | bytes 1572872 | tf_op jit(solution)/shard_map/ppermute | solution.py:76
  142.1 12.9 %collective-permute-start.12 = (f32[4,1,2,32,512]{4,3,1,2,0:T(8,128)S(1)}, f32[4,1,2,32,512]{4,3,1,2,0:T(8,128)S(1)}, u32[]{:S(2)}, u32[]{:S(2)}) collective-permute-start(f32[4,1,2,32,512]{4,3,1,2,0:T(8,128)S(1)} %slice_add_fusion.2), channel_id=1, source_target_pairs={{0,224},{32,0},{64,32},{96,64},{128,96},{160,128},{192,160},{224,1... | collective-permute-start | bytes 1572872 | tf_op jit(solution)/shard_map/ppermute | solution.py:77
  145.8 13.0 %collective-permute-start.5 = (f32[4,1,2,32,512]{4,3,1,2,0:T(8,128)S(1)}, f32[4,1,2,32,512]{4,3,1,2,0:T(8,128)S(1)}, u32[]{:S(2)}, u32[]{:S(2)}) collective-permute-start(f32[4,1,2,32,512]{4,3,1,2,0:T(8,128)S(1)} %slice_add_fusion.9), channel_id=1, source_target_pairs={{0,32},{32,64},{64,96},{96,128},{128,160},{160,192},{192,224},{224... | collective-permute-start | bytes 1572872 | tf_op jit(solution)/shard_map/ppermute | solution.py:76
  155.1 10.5 %collective-permute-start.13 = (f32[4,1,2,32,512]{4,3,1,2,0:T(8,128)S(1)}, f32[4,1,2,32,512]{4,3,1,2,0:T(8,128)S(1)}, u32[]{:S(2)}, u32[]{:S(2)}) collective-permute-start(f32[4,1,2,32,512]{4,3,1,2,0:T(8,128)S(1)} %slice_add_fusion.1), channel_id=1, source_target_pairs={{0,224},{32,0},{64,32},{96,64},{128,96},{160,128},{192,160},{224,1... | collective-permute-start | bytes 1572872 | tf_op jit(solution)/shard_map/ppermute | solution.py:77
  159.7 10.7 %collective-permute-start.6 = (f32[4,1,2,32,512]{4,3,1,2,0:T(8,128)}, f32[4,1,2,32,512]{4,3,1,2,0:T(8,128)}, u32[]{:S(2)}, u32[]{:S(2)}) collective-permute-start(f32[4,1,2,32,512]{4,3,1,2,0:T(8,128)} %slice_add_fusion.8), channel_id=1, source_target_pairs={{0,32},{32,64},{64,96},{96,128},{128,160},{160,192},{192,224},{224... | collective-permute-start | bytes 1572872 | tf_op jit(solution)/shard_map/ppermute | solution.py:76
  171.6 6.1 %collective-permute-start.14 = (f32[1,2,32,512]{3,2,1,0:T(8,128)S(1)}, f32[1,2,32,512]{3,2,1,0:T(8,128)S(1)}, u32[]{:S(2)}, u32[]{:S(2)}) collective-permute-start(f32[1,2,32,512]{3,2,1,0:T(8,128)S(1)} %get-tuple-element.27), channel_id=1, source_target_pairs={{0,8},{8,16},{16,24},{24,0},{1,9},{9,17},{17,25},{25,1},{2,10},{10... | collective-permute-start | bytes 393224 | tf_op jit(solution)/shard_map/ppermute | solution.py:76
  177.7 5.5 %collective-permute-start.15 = (f32[1,2,32,512]{3,2,1,0:T(8,128)S(1)}, f32[1,2,32,512]{3,2,1,0:T(8,128)S(1)}, u32[]{:S(2)}, u32[]{:S(2)}) collective-permute-start(f32[1,2,32,512]{3,2,1,0:T(8,128)S(1)} %fusion.48), channel_id=1, source_target_pairs={{0,8},{8,16},{16,24},{24,0},{1,9},{9,17},{17,25},{25,1},{2,10},{10... | collective-permute-start | bytes 393224 | tf_op jit(solution)/shard_map/ppermute | solution.py:76
  181.4 6.7 %collective-permute-start.17 = (f32[1,2,32,512]{3,2,1,0:T(8,128)S(1)}, f32[1,2,32,512]{3,2,1,0:T(8,128)S(1)}, u32[]{:S(2)}, u32[]{:S(2)}) collective-permute-start(f32[1,2,32,512]{3,2,1,0:T(8,128)S(1)} %get-tuple-element.28), channel_id=1, source_target_pairs={{0,24},{8,0},{16,8},{24,16},{1,25},{9,1},{17,9},{25,17},{2,26},{10... | collective-permute-start | bytes 393224 | tf_op jit(solution)/shard_map/ppermute | solution.py:77
  183.3 6.3 %collective-permute-start.16 = (f32[1,2,32,512]{3,2,1,0:T(8,128)S(1)}, f32[1,2,32,512]{3,2,1,0:T(8,128)S(1)}, u32[]{:S(2)}, u32[]{:S(2)}) collective-permute-start(f32[1,2,32,512]{3,2,1,0:T(8,128)S(1)} %fusion.53), channel_id=1, source_target_pairs={{0,8},{8,16},{16,24},{24,0},{1,9},{9,17},{17,25},{25,1},{2,10},{10... | collective-permute-start | bytes 393224 | tf_op jit(solution)/shard_map/ppermute | solution.py:76
  189.6 6.7 %collective-permute-start.18 = (f32[1,2,32,512]{3,2,1,0:T(8,128)S(1)}, f32[1,2,32,512]{3,2,1,0:T(8,128)S(1)}, u32[]{:S(2)}, u32[]{:S(2)}) collective-permute-start(f32[1,2,32,512]{3,2,1,0:T(8,128)S(1)} %get-tuple-element.26), channel_id=1, source_target_pairs={{0,24},{8,0},{16,8},{24,16},{1,25},{9,1},{17,9},{25,17},{2,26},{10... | collective-permute-start | bytes 393224 | tf_op jit(solution)/shard_map/ppermute | solution.py:77
  196.3 6.3 %collective-permute-start.19 = (f32[1,2,32,512]{3,2,1,0:T(8,128)S(1)}, f32[1,2,32,512]{3,2,1,0:T(8,128)S(1)}, u32[]{:S(2)}, u32[]{:S(2)}) collective-permute-start(f32[1,2,32,512]{3,2,1,0:T(8,128)S(1)} %fusion.56), channel_id=1, source_target_pairs={{0,24},{8,0},{16,8},{24,16},{1,25},{9,1},{17,9},{25,17},{2,26},{10... | collective-permute-start | bytes 393224 | tf_op jit(solution)/shard_map/ppermute | solution.py:77
  203.5 11.1 %all-to-all-start.2 = ((f32[2,2,32,512]{3,1,0,2:T(2,128)}), f32[2,2,32,512]{3,1,0,2:T(2,128)S(1)}, u32[]{:S(2)}, u32[]{:S(2)}) async-start(f32[2,2,32,512]{3,1,0,2:T(2,128)} %copy.43), calls=%async_computation.2 | async-start | bytes 524288 | tf_op jit(solution)/shard_map/all_to_all | solution.py:98
  (2 other events, 37.4 us)

commit v2 on v0

--- a/solution.py
+++ b/solution.py
@@ -60,9 +60,8 @@
     return dedisperse
 
 
-def ring_reduce_scatter(chunks, axis, size, split_axis):
+def ring_reduce_scatter(halves, axis, size):
     position = lax.axis_index(axis)
-    halves = jnp.split(chunks, 2, axis=split_axis)
     forward = [(i, (i + 1) % size) for i in range(size)]
     backward = [(i, (i - 1) % size) for i in range(size)]
 
@@ -74,7 +73,7 @@
     for step in range(size - 1):
         acc_cw = lax.ppermute(acc_cw, axis, forward) + pick(halves[0], position - step - 2)
         acc_ccw = lax.ppermute(acc_ccw, axis, backward) + pick(halves[1], position + step + 2)
-    return jnp.concatenate([acc_cw, acc_ccw], axis=split_axis - 1)
+    return acc_cw, acc_ccw
 
 
 def on_device(voltages, weights, channel_map, sweep_response_taps, chirp_length):
@@ -85,14 +84,15 @@
     local_weights = lax.all_to_all(weights, ("z", "x"), split_axis=4, concat_axis=0, tiled=True)
     local_weights = local_weights.reshape((zs, xs) + local_weights.shape[1:])
     mixing = mixing_matrix(local_weights, 2)
-    partial = jnp.einsum(
-        "zxopbra,rpzxat->zxopbt",
-        mixing,
-        own,
-        preferred_element_type=jnp.float32,
-    )
-    partial = ring_reduce_scatter(partial, "z", zs, 2)
-    beams = ring_reduce_scatter(partial, "x", xs, 1)
+    parts = [
+        jnp.einsum(
+            "zxpbra,rpzxat->zxpbt", mixing[:, :, o], own, preferred_element_type=jnp.float32
+        )
+        for o in range(2)
+    ]
+    parts = ring_reduce_scatter(parts, "z", zs)
+    parts = ring_reduce_scatter(parts, "x", xs)
+    beams = jnp.stack(parts, axis=0)
     dedisperse = build_dedispersion(sweep_response_taps, chirp_length)
     result = dedisperse(lax.all_to_all(beams, "tm", split_axis=2, concat_axis=3, tiled=True))
     return result[None]

time: 217 us -> 206 us (0.949)
  local copies, waits for them, and re-layouts: 45.4 us -> 39.5 us
  waiting for transfers between devices: 78.5 us -> 76.1 us
    ppermute x10, waiting for transfers between devices: 42.1 us -> 25.6 us  [ring_reduce_scatter(): lax.ppermute(acc_cw, axis, forward) + pick(halves[0], position - step - 2)]
    ppermute x10, waiting for transfers between devices: 17.8 us -> 32.1 us  [ring_reduce_scatter(): lax.ppermute(acc_ccw, axis, backward) + pick(halves[1], position + step + 2)]
    split x1 -> x0, local copies, waits for them, and re-layouts: 6.92 us -> none  [ring_reduce_scatter(): halves = jnp.split(chunks, 2, axis=split_axis)]
    add x10 -> x9, other arithmetic: 10.2 us -> 8.13 us  [ring_reduce_scatter(): lax.ppermute(acc_cw, axis, forward) + pick(halves[0], position - step - 2)]
    unnamed x13 -> x19, local copies, waits for them, and re-layouts: 7.29 us -> 9.28 us
    dot_general x1 -> x2, matrix products: 8.06 us -> 6.11 us  [on_device(): jnp.einsum('zxpbra,rpzxat->zxpbt', mixing[:, :, o], own, preferred_elemen...]
    add x10 -> x9, other arithmetic: 8.27 us -> 10 us  [ring_reduce_scatter(): lax.ppermute(acc_ccw, axis, backward) + pick(halves[1], position + step + 2)]
  transfers between devices with their start and end apart: 23 -> 23, of which waited for: 15 -> 19; matrix products, arithmetic and copies ran while one was open for 17% -> 18% of each run, Pallas kernels for 0% -> 0%
where the time goes in v2:
time: 206 us; the launch traced here: 204 us
  waiting for transfers between devices  76.1 us (37%)
  starting transfers between devices  53.2 us (26%)
  local copies, waits for them, and re-layouts  39.5 us (19%)
  other arithmetic  24.1 us (12%)
  matrix products  9.98 us (5%)
    ppermute x10, waiting for transfers between devices, ring_reduce_scatter(): lax.ppermute(acc_ccw, axis, backward) + pick(halves[1], position + step + 2)  32.1 us
    ppermute x10, waiting for transfers between devices, ring_reduce_scatter(): lax.ppermute(acc_cw, axis, forward) + pick(halves[0], position - step - 2)  25.6 us
    ppermute x10, starting transfers between devices, ring_reduce_scatter(): lax.ppermute(acc_ccw, axis, backward) + pick(halves[1], position + step + 2)  23 us
    gather x2, local copies, waits for them, and re-layouts, on_device(): jnp.take(voltages, order, axis=2, mode='clip')  17.3 us
    all_to_all x1, starting transfers between devices, on_device(): lax.all_to_all(weights, ('z', 'x'), split_axis=4, concat_axis=0, tiled=True)  11.6 us
    add x9, other arithmetic, ring_reduce_scatter(): lax.ppermute(acc_ccw, axis, backward) + pick(halves[1], position + step + 2)  10 us
    unnamed x19, local copies, waits for them, and re-layouts  9.28 us
    all_to_all x1, waiting for transfers between devices, on_device(): lax.all_to_all(weights, ('z', 'x'), split_axis=4, concat_axis=0, tiled=True)  8.8 us
  transfers between devices with their start and end apart: 23, of which 19 were waited for; matrix products, arithmetic and copies ran while one was open for 18% of the time, Pallas kernels for 0%

profile of v2, /device:TPU:6, one launch (start us, length us, event | category | flops | bytes accessed | tf_op | source)
XLA Modules:
  0.0 203.6 jit_solution(12206074358327233743)
XLA Ops:
  1.0 9.0 %gather_fusion = bf16[64,2,2,32,512]{4,3,2,1,0:T(8,128)(2,1)} fusion(bf16[2,2,64,32,512]{4,3,2,1,0:T(8,128)(2,1)} %param.5, s32[1024]{0:T(1024)S(1)} %pad_clamp_fusion), kind=kCustom, calls=%fused_computation | custom fusion | bytes 16777472 | tf_op jit(solution)/shard_map/jit(_take)/gather | solution.py:82
  10.0 8.3 %copy.16 = bf16[64,2,2,32,512]{4,3,1,2,0:T(8,128)(2,1)} copy(bf16[64,2,2,32,512]{4,3,2,1,0:T(8,128)(2,1)} %gather_fusion) | data formatting | bytes 16777216 | tf_op jit(solution)/shard_map/jit(_take)/gather | solution.py:82
  18.3 7.1 %all-to-all-start.1 = ((bf16[2,2,2,8,4,32,512]{6,5,1,2,4,3,0:T(8,128)(2,1)}), bf16[2,2,2,8,4,32,512]{6,5,1,2,4,3,0:T(8,128)(2,1)}, u32[]{:S(2)}, u32[]{:S(2)}) async-start(bf16[2,2,2,8,4,32,512]{6,5,1,2,4,3,0:T(8,128)(2,1)} %bitcast.154), calls=%async_computation.1 | async-start | bytes 16777216 | tf_op jit(solution)/shard_map/all_to_all | solution.py:83
  29.6 3.3 %all-to-all-done.1 = bf16[2,2,2,8,4,32,512]{6,5,1,2,4,3,0:T(8,128)(2,1)} async-done(((bf16[2,2,2,8,4,32,512]{6,5,1,2,4,3,0:T(8,128)(2,1)}), bf16[2,2,2,8,4,32,512]{6,5,1,2,4,3,0:T(8,128)(2,1)}, u32[]{:S(2)}, u32[]{:S(2)}) %all-to-all-start.1) | async-done | bytes 8388640 | tf_op jit(solution)/shard_map/all_to_all | solution.py:83
  32.9 11.6 %all-to-all-start = ((bf16[32,2,4096]{2,1,0:T(2,128)(2,1)}), bf16[32,2,4096]{2,1,0:T(2,128)(2,1)S(1)}, u32[]{:S(2)}, u32[]{:S(2)}) async-start(bf16[32,2,4096]{2,1,0:T(2,128)(2,1)} %reshape.53), calls=%async_computation | async-start | bytes 1048576 | tf_op jit(solution)/shard_map/all_to_all | solution.py:84
  44.5 8.3 %copy.17 = bf16[1,2,2,8,4,2,32,512]{7,6,5,1,2,4,3,0:T(8,128)(2,1)} copy(bf16[1,2,2,8,4,2,32,512]{7,6,1,2,4,3,5,0:T(8,128)(2,1)} %bitcast.10) | data formatting | bytes 16777216 | tf_op jit(solution)/shard_map/all_to_all | solution.py:83
  52.8 8.8 %all-to-all-done = bf16[32,2,4096]{2,1,0:T(2,128)(2,1)S(1)} async-done(((bf16[32,2,4096]{2,1,0:T(2,128)(2,1)}), bf16[32,2,4096]{2,1,0:T(2,128)(2,1)S(1)}, u32[]{:S(2)}, u32[]{:S(2)}) %all-to-all-start) | async-done | bytes 524320 | tf_op jit(solution)/shard_map/all_to_all | solution.py:84
  65.5 4.8 %convolution_bitcast_fusion = f32[8,4,2,32,512]{4,3,2,1,0:T(8,128)S(1)} fusion(bf16[2,2,8,4,64,512]{5,4,0,1,3,2:T(8,128)(2,1)} %bitcast.150, bf16[8,4,2,32,1,64]{5,3,4,2,1,0:T(8,128)(2,1)S(1)} %get-tuple-element.10, bf16[8,4,2,32,1,64]{5,3,4,2,1,0:T(8,128)(2,1)S(1)} %get-tuple-element.9), kind=kOutput, calls=%fused_computation.1 | convolution fusion | flops 268697600 | bytes 13107200 | tf_op jit(solution)/shard_map/zxpbra,rpzxat->zxpbt/dot_general | solution.py:88
  77.8 7.0 %collective-permute-done.10 = f32[4,2,32,512]{3,2,1,0:T(8,128)S(1)} collective-permute-done((f32[4,2,32,512]{3,2,1,0:T(8,128)S(1)}, f32[4,2,32,512]{3,2,1,0:T(8,128)S(1)}, u32[]{:S(2)}, u32[]{:S(2)}) %collective-permute-start.10) | collective-permute-done | bytes 524320 | tf_op jit(solution)/shard_map/ppermute | solution.py:75
  91.2 6.4 %collective-permute-done.11 = f32[4,2,32,512]{3,2,1,0:T(8,128)S(1)} collective-permute-done((f32[4,2,32,512]{3,2,1,0:T(8,128)S(1)}, f32[4,2,32,512]{3,2,1,0:T(8,128)S(1)}, u32[]{:S(2)}, u32[]{:S(2)}) %collective-permute-start.11) | collective-permute-done | bytes 524320 | tf_op jit(solution)/shard_map/ppermute | solution.py:75
  98.8 3.2 %collective-permute-start.12 = (f32[4,2,32,512]{3,2,1,0:T(8,128)S(1)}, f32[4,2,32,512]{3,2,1,0:T(8,128)S(1)}, u32[]{:S(2)}, u32[]{:S(2)}) collective-permute-start(f32[4,2,32,512]{3,2,1,0:T(8,128)S(1)} %bitcast_add_fusion.5), channel_id=1, source_target_pairs={{0,224},{32,0},{64,32},{96,64},{128,96},{160,128},{192,160},{224,1... | collective-permute-start | bytes 1572872 | tf_op jit(solution)/shard_map/ppermute | solution.py:75
  104.7 5.8 %collective-permute-done.12 = f32[4,2,32,512]{3,2,1,0:T(8,128)S(1)} collective-permute-done((f32[4,2,32,512]{3,2,1,0:T(8,128)S(1)}, f32[4,2,32,512]{3,2,1,0:T(8,128)S(1)}, u32[]{:S(2)}, u32[]{:S(2)}) %collective-permute-start.12) | collective-permute-done | bytes 524320 | tf_op jit(solution)/shard_map/ppermute | solution.py:75
  111.7 3.8 %collective-permute-start.13 = (f32[4,2,32,512]{3,2,1,0:T(8,128)S(1)}, f32[4,2,32,512]{3,2,1,0:T(8,128)S(1)}, u32[]{:S(2)}, u32[]{:S(2)}) collective-permute-start(f32[4,2,32,512]{3,2,1,0:T(8,128)S(1)} %bitcast_add_fusion.4), channel_id=1, source_target_pairs={{0,224},{32,0},{64,32},{96,64},{128,96},{160,128},{192,160},{224,1... | collective-permute-start | bytes 1572872 | tf_op jit(solution)/shard_map/ppermute | solution.py:75
  117.9 5.2 %collective-permute-done.13 = f32[4,2,32,512]{3,2,1,0:T(8,128)S(1)} collective-permute-done((f32[4,2,32,512]{3,2,1,0:T(8,128)S(1)}, f32[4,2,32,512]{3,2,1,0:T(8,128)S(1)}, u32[]{:S(2)}, u32[]{:S(2)}) %collective-permute-start.13) | collective-permute-done | bytes 524320 | tf_op jit(solution)/shard_map/ppermute | solution.py:75
  124.3 3.8 %collective-permute-start.14 = (f32[4,2,32,512]{3,2,1,0:T(8,128)S(1)}, f32[4,2,32,512]{3,2,1,0:T(8,128)S(1)}, u32[]{:S(2)}, u32[]{:S(2)}) collective-permute-start(f32[4,2,32,512]{3,2,1,0:T(8,128)S(1)} %bitcast_add_fusion.3), channel_id=1, source_target_pairs={{0,224},{32,0},{64,32},{96,64},{128,96},{160,128},{192,160},{224,1... | collective-permute-start | bytes 1572872 | tf_op jit(solution)/shard_map/ppermute | solution.py:75
  130.3 4.6 %collective-permute-done.14 = f32[4,2,32,512]{3,2,1,0:T(8,128)S(1)} collective-permute-done((f32[4,2,32,512]{3,2,1,0:T(8,128)S(1)}, f32[4,2,32,512]{3,2,1,0:T(8,128)S(1)}, u32[]{:S(2)}, u32[]{:S(2)}) %collective-permute-start.14) | collective-permute-done | bytes 524320 | tf_op jit(solution)/shard_map/ppermute | solution.py:75
  136.8 3.7 %collective-permute-start.15 = (f32[4,2,32,512]{3,2,1,0:T(8,128)}, f32[4,2,32,512]{3,2,1,0:T(8,128)}, u32[]{:S(2)}, u32[]{:S(2)}) collective-permute-start(f32[4,2,32,512]{3,2,1,0:T(8,128)} %bitcast_add_fusion.2), channel_id=1, source_target_pairs={{0,224},{32,0},{64,32},{96,64},{128,96},{160,128},{192,160},{224,1... | collective-permute-start | bytes 1572872 | tf_op jit(solution)/shard_map/ppermute | solution.py:75
  140.5 4.1 %fusion.26 = (f32[512,512]{1,0:T(8,128)S(1)}, f32[512,512]{1,0:T(8,128)S(1)}) fusion(), kind=kLoop, calls=%fused_computation.54 | loop fusion | flops 3670016 | bytes 2097152 | tf_op jit(solution)/shard_map/sin | solution.py:21
  149.9 3.7 %collective-permute-start.16 = (f32[4,2,32,512]{3,2,1,0:T(8,128)}, f32[4,2,32,512]{3,2,1,0:T(8,128)}, u32[]{:S(2)}, u32[]{:S(2)}) collective-permute-start(f32[4,2,32,512]{3,2,1,0:T(8,128)} %bitcast_add_fusion.1), channel_id=1, source_target_pairs={{0,224},{32,0},{64,32},{96,64},{128,96},{160,128},{192,160},{224,1... | collective-permute-start | bytes 1572872 | tf_op jit(solution)/shard_map/ppermute | solution.py:75
  153.9 3.9 %collective-permute-done.5 = f32[4,2,32,512]{3,2,1,0:T(8,128)S(1)} collective-permute-done((f32[4,2,32,512]{3,2,1,0:T(8,128)S(1)}, f32[4,2,32,512]{3,2,1,0:T(8,128)S(1)}, u32[]{:S(2)}, u32[]{:S(2)}) %collective-permute-start.5) | collective-permute-done | bytes 524320 | tf_op jit(solution)/shard_map/ppermute | solution.py:74
  162.6 7.1 %collective-permute-done.6 = f32[4,2,32,512]{3,2,1,0:T(8,128)S(1)} collective-permute-done((f32[4,2,32,512]{3,2,1,0:T(8,128)S(1)}, f32[4,2,32,512]{3,2,1,0:T(8,128)S(1)}, u32[]{:S(2)}, u32[]{:S(2)}) %collective-permute-start.6) | collective-permute-done | bytes 524320 | tf_op jit(solution)/shard_map/ppermute | solution.py:74
  173.2 3.6 %collective-permute-done.7 = f32[2,32,512]{2,0,1:T(2,128)S(1)} collective-permute-done((f32[2,32,512]{2,0,1:T(2,128)S(1)}, f32[2,32,512]{2,0,1:T(2,128)S(1)}, u32[]{:S(2)}, u32[]{:S(2)}) %collective-permute-start.7) | collective-permute-done | bytes 131104 | tf_op jit(solution)/shard_map/ppermute | solution.py:74
  188.2 4.5 %all-to-all-start.2 = ((f32[2,2,32,512]{3,1,0,2:T(2,128)}), f32[2,2,32,512]{3,1,0,2:T(2,128)S(1)}, u32[]{:S(2)}, u32[]{:S(2)}) async-start(f32[2,2,32,512]{3,1,0,2:T(2,128)} %pad_maximum_fusion), calls=%async_computation.2 | async-start | bytes 524288 | tf_op jit(solution)/shard_map/all_to_all | solution.py:97
  192.9 6.4 %all-to-all-done.2 = f32[2,2,32,512]{3,1,0,2:T(2,128)S(1)} async-done(((f32[2,2,32,512]{3,1,0,2:T(2,128)}), f32[2,2,32,512]{3,1,0,2:T(2,128)S(1)}, u32[]{:S(2)}, u32[]{:S(2)}) %all-to-all-start.2) | async-done | bytes 262176 | tf_op jit(solution)/shard_map/all_to_all | solution.py:97
  (103 shorter events, 65.0 us)
Async XLA Ops:
  18.3 14.6 %all-to-all-start.1 = ((bf16[2,2,2,8,4,32,512]{6,5,1,2,4,3,0:T(8,128)(2,1)}), bf16[2,2,2,8,4,32,512]{6,5,1,2,4,3,0:T(8,128)(2,1)}, u32[]{:S(2)}, u32[]{:S(2)}) async-start(bf16[2,2,2,8,4,32,512]{6,5,1,2,4,3,0:T(8,128)(2,1)} %bitcast.154), calls=%async_computation.1 | async-start | bytes 16777216 | tf_op jit(solution)/shard_map/all_to_all | solution.py:83
  32.9 28.7 %all-to-all-start = ((bf16[32,2,4096]{2,1,0:T(2,128)(2,1)}), bf16[32,2,4096]{2,1,0:T(2,128)(2,1)S(1)}, u32[]{:S(2)}, u32[]{:S(2)}) async-start(bf16[32,2,4096]{2,1,0:T(2,128)(2,1)} %reshape.53), calls=%async_computation | async-start | bytes 1048576 | tf_op jit(solution)/shard_map/all_to_all | solution.py:84
  72.3 12.5 %collective-permute-start.10 = (f32[4,2,32,512]{3,2,1,0:T(8,128)S(1)}, f32[4,2,32,512]{3,2,1,0:T(8,128)S(1)}, u32[]{:S(2)}, u32[]{:S(2)}) collective-permute-start(f32[4,2,32,512]{3,2,1,0:T(8,128)S(1)} %dynamic-slice_bitcast_fusion), channel_id=1, source_target_pairs={{0,224},{32,0},{64,32},{96,64},{128,96},{160,128},{192,160},{224,1... | collective-permute-start | bytes 1572872 | tf_op jit(solution)/shard_map/ppermute | solution.py:75
  75.7 13.8 %collective-permute-start = (f32[4,2,32,512]{3,2,1,0:T(8,128)S(1)}, f32[4,2,32,512]{3,2,1,0:T(8,128)S(1)}, u32[]{:S(2)}, u32[]{:S(2)}) collective-permute-start(f32[4,2,32,512]{3,2,1,0:T(8,128)S(1)} %dynamic-slice_bitcast_fusion.1), channel_id=1, source_target_pairs={{0,32},{32,64},{64,96},{96,128},{128,160},{160,192},{192,224},{224... | collective-permute-start | bytes 1572872 | tf_op jit(solution)/shard_map/ppermute | solution.py:74
  85.9 11.7 %collective-permute-start.11 = (f32[4,2,32,512]{3,2,1,0:T(8,128)S(1)}, f32[4,2,32,512]{3,2,1,0:T(8,128)S(1)}, u32[]{:S(2)}, u32[]{:S(2)}) collective-permute-start(f32[4,2,32,512]{3,2,1,0:T(8,128)S(1)} %bitcast_add_fusion.6), channel_id=1, source_target_pairs={{0,224},{32,0},{64,32},{96,64},{128,96},{160,128},{192,160},{224,1... | collective-permute-start | bytes 1572872 | tf_op jit(solution)/shard_map/ppermute | solution.py:75
  90.6 12.9 %collective-permute-start.1 = (f32[4,2,32,512]{3,2,1,0:T(8,128)S(1)}, f32[4,2,32,512]{3,2,1,0:T(8,128)S(1)}, u32[]{:S(2)}, u32[]{:S(2)}) collective-permute-start(f32[4,2,32,512]{3,2,1,0:T(8,128)S(1)} %bitcast_add_fusion.13), channel_id=1, source_target_pairs={{0,32},{32,64},{64,96},{96,128},{128,160},{160,192},{192,224},{224... | collective-permute-start | bytes 1572872 | tf_op jit(solution)/shard_map/ppermute | solution.py:74
  98.8 31.5 %copy-start.4 = (s32[8]{0:T(128)S(1)}, s32[8]{0:T(128)}, u32[]{:S(2)}) copy-start(s32[8]{0:T(128)} %param.9) | copy-start | bytes 100
  98.8 11.8 %collective-permute-start.12 = (f32[4,2,32,512]{3,2,1,0:T(8,128)S(1)}, f32[4,2,32,512]{3,2,1,0:T(8,128)S(1)}, u32[]{:S(2)}, u32[]{:S(2)}) collective-permute-start(f32[4,2,32,512]{3,2,1,0:T(8,128)S(1)} %bitcast_add_fusion.5), channel_id=1, source_target_pairs={{0,224},{32,0},{64,32},{96,64},{128,96},{160,128},{192,160},{224,1... | collective-permute-start | bytes 1572872 | tf_op jit(solution)/shard_map/ppermute | solution.py:75
  104.6 12.1 %collective-permute-start.2 = (f32[4,2,32,512]{3,2,1,0:T(8,128)S(1)}, f32[4,2,32,512]{3,2,1,0:T(8,128)S(1)}, u32[]{:S(2)}, u32[]{:S(2)}) collective-permute-start(f32[4,2,32,512]{3,2,1,0:T(8,128)S(1)} %bitcast_add_fusion.12), channel_id=1, source_target_pairs={{0,32},{32,64},{64,96},{96,128},{128,160},{160,192},{192,224},{224... | collective-permute-start | bytes 1572872 | tf_op jit(solution)/shard_map/ppermute | solution.py:74
  111.7 11.5 %collective-permute-start.13 = (f32[4,2,32,512]{3,2,1,0:T(8,128)S(1)}, f32[4,2,32,512]{3,2,1,0:T(8,128)S(1)}, u32[]{:S(2)}, u32[]{:S(2)}) collective-permute-start(f32[4,2,32,512]{3,2,1,0:T(8,128)S(1)} %bitcast_add_fusion.4), channel_id=1, source_target_pairs={{0,224},{32,0},{64,32},{96,64},{128,96},{160,128},{192,160},{224,1... | collective-permute-start | bytes 1572872 | tf_op jit(solution)/shard_map/ppermute | solution.py:75
  117.8 11.2 %collective-permute-start.3 = (f32[4,2,32,512]{3,2,1,0:T(8,128)S(1)}, f32[4,2,32,512]{3,2,1,0:T(8,128)S(1)}, u32[]{:S(2)}, u32[]{:S(2)}) collective-permute-start(f32[4,2,32,512]{3,2,1,0:T(8,128)S(1)} %bitcast_add_fusion.11), channel_id=1, source_target_pairs={{0,32},{32,64},{64,96},{96,128},{128,160},{160,192},{192,224},{224... | collective-permute-start | bytes 1572872 | tf_op jit(solution)/shard_map/ppermute | solution.py:74
  124.3 10.6 %collective-permute-start.14 = (f32[4,2,32,512]{3,2,1,0:T(8,128)S(1)}, f32[4,2,32,512]{3,2,1,0:T(8,128)S(1)}, u32[]{:S(2)}, u32[]{:S(2)}) collective-permute-start(f32[4,2,32,512]{3,2,1,0:T(8,128)S(1)} %bitcast_add_fusion.3), channel_id=1, source_target_pairs={{0,224},{32,0},{64,32},{96,64},{128,96},{160,128},{192,160},{224,1... | collective-permute-start | bytes 1572872 | tf_op jit(solution)/shard_map/ppermute | solution.py:75
  130.1 14.5 %collective-permute-start.4 = (f32[4,2,32,512]{3,2,1,0:T(8,128)S(1)}, f32[4,2,32,512]{3,2,1,0:T(8,128)S(1)}, u32[]{:S(2)}, u32[]{:S(2)}) collective-permute-start(f32[4,2,32,512]{3,2,1,0:T(8,128)S(1)} %bitcast_add_fusion.10), channel_id=1, source_target_pairs={{0,32},{32,64},{64,96},{96,128},{128,160},{160,192},{192,224},{224... | collective-permute-start | bytes 1572872 | tf_op jit(solution)/shard_map/ppermute | solution.py:74
  136.8 11.0 %collective-permute-start.15 = (f32[4,2,32,512]{3,2,1,0:T(8,128)}, f32[4,2,32,512]{3,2,1,0:T(8,128)}, u32[]{:S(2)}, u32[]{:S(2)}) collective-permute-start(f32[4,2,32,512]{3,2,1,0:T(8,128)} %bitcast_add_fusion.2), channel_id=1, source_target_pairs={{0,224},{32,0},{64,32},{96,64},{128,96},{160,128},{192,160},{224,1... | collective-permute-start | bytes 1572872 | tf_op jit(solution)/shard_map/ppermute | solution.py:75
  145.8 12.0 %collective-permute-start.5 = (f32[4,2,32,512]{3,2,1,0:T(8,128)S(1)}, f32[4,2,32,512]{3,2,1,0:T(8,128)S(1)}, u32[]{:S(2)}, u32[]{:S(2)}) collective-permute-start(f32[4,2,32,512]{3,2,1,0:T(8,128)S(1)} %bitcast_add_fusion.9), channel_id=1, source_target_pairs={{0,32},{32,64},{64,96},{96,128},{128,160},{160,192},{192,224},{224... | collective-permute-start | bytes 1572872 | tf_op jit(solution)/shard_map/ppermute | solution.py:74
  149.9 10.7 %collective-permute-start.16 = (f32[4,2,32,512]{3,2,1,0:T(8,128)}, f32[4,2,32,512]{3,2,1,0:T(8,128)}, u32[]{:S(2)}, u32[]{:S(2)}) collective-permute-start(f32[4,2,32,512]{3,2,1,0:T(8,128)} %bitcast_add_fusion.1), channel_id=1, source_target_pairs={{0,224},{32,0},{64,32},{96,64},{128,96},{160,128},{192,160},{224,1... | collective-permute-start | bytes 1572872 | tf_op jit(solution)/shard_map/ppermute | solution.py:75
  158.9 10.7 %collective-permute-start.6 = (f32[4,2,32,512]{3,2,1,0:T(8,128)S(1)}, f32[4,2,32,512]{3,2,1,0:T(8,128)S(1)}, u32[]{:S(2)}, u32[]{:S(2)}) collective-permute-start(f32[4,2,32,512]{3,2,1,0:T(8,128)S(1)} %bitcast_add_fusion.8), channel_id=1, source_target_pairs={{0,32},{32,64},{64,96},{96,128},{128,160},{160,192},{192,224},{224... | collective-permute-start | bytes 1572872 | tf_op jit(solution)/shard_map/ppermute | solution.py:74
  162.1 9.5 %collective-permute-start.17 = (f32[2,32,512]{2,0,1:T(2,128)S(1)}, f32[2,32,512]{2,0,1:T(2,128)S(1)}, u32[]{:S(2)}, u32[]{:S(2)}) collective-permute-start(f32[2,32,512]{2,0,1:T(2,128)S(1)} %bitcast.163), channel_id=1, source_target_pairs={{0,24},{8,0},{16,8},{24,16},{1,25},{9,1},{17,9},{25,17},{2,26},{10... | collective-permute-start | bytes 393224 | tf_op jit(solution)/shard_map/ppermute | solution.py:75
  170.9 5.9 %collective-permute-start.7 = (f32[2,32,512]{2,0,1:T(2,128)S(1)}, f32[2,32,512]{2,0,1:T(2,128)S(1)}, u32[]{:S(2)}, u32[]{:S(2)}) collective-permute-start(f32[2,32,512]{2,0,1:T(2,128)S(1)} %bitcast.164), channel_id=1, source_target_pairs={{0,8},{8,16},{16,24},{24,0},{1,9},{9,17},{17,25},{25,1},{2,10},{10... | collective-permute-start | bytes 393224 | tf_op jit(solution)/shard_map/ppermute | solution.py:74
  171.7 6.3 %collective-permute-start.18 = (f32[2,32,512]{2,0,1:T(2,128)S(1)}, f32[2,32,512]{2,0,1:T(2,128)S(1)}, u32[]{:S(2)}, u32[]{:S(2)}) collective-permute-start(f32[2,32,512]{2,0,1:T(2,128)S(1)} %bitcast_add_fusion.16), channel_id=1, source_target_pairs={{0,24},{8,0},{16,8},{24,16},{1,25},{9,1},{17,9},{25,17},{2,26},{10... | collective-permute-start | bytes 393224 | tf_op jit(solution)/shard_map/ppermute | solution.py:75
  177.0 5.0 %collective-permute-start.8 = (f32[2,32,512]{2,0,1:T(2,128)S(1)}, f32[2,32,512]{2,0,1:T(2,128)S(1)}, u32[]{:S(2)}, u32[]{:S(2)}) collective-permute-start(f32[2,32,512]{2,0,1:T(2,128)S(1)} %bitcast_add_fusion.19), channel_id=1, source_target_pairs={{0,8},{8,16},{16,24},{24,0},{1,9},{9,17},{17,25},{25,1},{2,10},{10... | collective-permute-start | bytes 393224 | tf_op jit(solution)/shard_map/ppermute | solution.py:74
  178.1 6.3 %collective-permute-start.19 = (f32[2,32,512]{2,0,1:T(2,128)S(1)}, f32[2,32,512]{2,0,1:T(2,128)S(1)}, u32[]{:S(2)}, u32[]{:S(2)}) collective-permute-start(f32[2,32,512]{2,0,1:T(2,128)S(1)} %bitcast_add_fusion.15), channel_id=1, source_target_pairs={{0,24},{8,0},{16,8},{24,16},{1,25},{9,1},{17,9},{25,17},{2,26},{10... | collective-permute-start | bytes 393224 | tf_op jit(solution)/shard_map/ppermute | solution.py:75
  182.1 5.0 %collective-permute-start.9 = (f32[2,32,512]{2,0,1:T(2,128)S(1)}, f32[2,32,512]{2,0,1:T(2,128)S(1)}, u32[]{:S(2)}, u32[]{:S(2)}) collective-permute-start(f32[2,32,512]{2,0,1:T(2,128)S(1)} %bitcast_add_fusion.18), channel_id=1, source_target_pairs={{0,8},{8,16},{16,24},{24,0},{1,9},{9,17},{17,25},{25,1},{2,10},{10... | collective-permute-start | bytes 393224 | tf_op jit(solution)/shard_map/ppermute | solution.py:74
  188.2 11.2 %all-to-all-start.2 = ((f32[2,2,32,512]{3,1,0,2:T(2,128)}), f32[2,2,32,512]{3,1,0,2:T(2,128)S(1)}, u32[]{:S(2)}, u32[]{:S(2)}) async-start(f32[2,2,32,512]{3,1,0,2:T(2,128)} %pad_maximum_fusion), calls=%async_computation.2 | async-start | bytes 524288 | tf_op jit(solution)/shard_map/all_to_all | solution.py:97
  (6 other events, 52.8 us)

commit v3 on v2

--- a/solution.py
+++ b/solution.py
@@ -81,7 +81,10 @@
     order = channel_map.reshape(zs, xs, cs).transpose(2, 0, 1)
     selected = jnp.moveaxis(jnp.take(voltages, order, axis=2, mode="clip"), 2, 0)
     own = lax.all_to_all(selected, "c", split_axis=0, concat_axis=5, tiled=True)[0]
-    local_weights = lax.all_to_all(weights, ("z", "x"), split_axis=4, concat_axis=0, tiled=True)
+    groups = zs * xs
+    grouped = weights[0].reshape(weights.shape[1:4] + (groups, -1))
+    grouped = jnp.moveaxis(grouped, 3, 0)
+    local_weights = lax.all_to_all(grouped, ("z", "x"), split_axis=0, concat_axis=0, tiled=True)
     local_weights = local_weights.reshape((zs, xs) + local_weights.shape[1:])
     mixing = mixing_matrix(local_weights, 2)
     parts = [

time: 206 us -> 203 us (0.985)
  local copies, waits for them, and re-layouts: 39.5 us -> 35.3 us
    unnamed x19 -> x18, local copies, waits for them, and re-layouts: 9.28 us -> 6.27 us
    all_to_all x1, local copies, waits for them, and re-layouts: 2.73 us -> 0.08 us  [on_device(): lax.all_to_all(grouped, ('z', 'x'), split_axis=0, concat_axis=0, tiled=True)]
where the time goes in v3:
time: 203 us; the launch traced here: 200 us
  waiting for transfers between devices  77.3 us (38%)
  starting transfers between devices  53 us (26%)
  local copies, waits for them, and re-layouts  35.3 us (17%)
  other arithmetic  24.1 us (12%)
  matrix products  9.98 us (5%)
    ppermute x10, waiting for transfers between devices, ring_reduce_scatter(): lax.ppermute(acc_ccw, axis, backward) + pick(halves[1], position + step + 2)  30.7 us
    ppermute x10, waiting for transfers between devices, ring_reduce_scatter(): lax.ppermute(acc_cw, axis, forward) + pick(halves[0], position - step - 2)  27 us
    ppermute x10, starting transfers between devices, ring_reduce_scatter(): lax.ppermute(acc_ccw, axis, backward) + pick(halves[1], position + step + 2)  22.8 us
    gather x2, local copies, waits for them, and re-layouts, on_device(): jnp.take(voltages, order, axis=2, mode='clip')  17.3 us
    all_to_all x1, starting transfers between devices, on_device(): lax.all_to_all(grouped, ('z', 'x'), split_axis=0, concat_axis=0, tiled=True)  11.6 us
    add x9, other arithmetic, ring_reduce_scatter(): lax.ppermute(acc_ccw, axis, backward) + pick(halves[1], position + step + 2)  10 us
    all_to_all x1, waiting for transfers between devices, on_device(): lax.all_to_all(grouped, ('z', 'x'), split_axis=0, concat_axis=0, tiled=True)  8.8 us
    all_to_all x1, local copies, waits for them, and re-layouts, on_device(): lax.all_to_all(selected, 'c', split_axis=0, concat_axis=5, tiled=True)[0]  8.29 us
  transfers between devices with their start and end apart: 23, of which 19 were waited for; matrix products, arithmetic and copies ran while one was open for 18% of the time, Pallas kernels for 0%

profile of v3, /device:TPU:6, one launch (start us, length us, event | category | flops | bytes accessed | tf_op | source)
XLA Modules:
  0.0 200.4 jit_solution(15533199122505987777)
XLA Ops:
  1.0 9.0 %gather_fusion = bf16[64,2,2,32,512]{4,3,2,1,0:T(8,128)(2,1)} fusion(bf16[2,2,64,32,512]{4,3,2,1,0:T(8,128)(2,1)} %param.5, s32[1024]{0:T(1024)S(1)} %pad_clamp_fusion), kind=kCustom, calls=%fused_computation | custom fusion | bytes 16777472 | tf_op jit(solution)/shard_map/jit(_take)/gather | solution.py:82
  10.0 8.3 %copy.30 = bf16[64,2,2,32,512]{4,3,1,2,0:T(8,128)(2,1)} copy(bf16[64,2,2,32,512]{4,3,2,1,0:T(8,128)(2,1)} %gather_fusion) | data formatting | bytes 16777216 | tf_op jit(solution)/shard_map/jit(_take)/gather | solution.py:82
  18.3 7.1 %all-to-all-start.1 = ((bf16[2,2,2,8,4,32,512]{6,5,1,2,4,3,0:T(8,128)(2,1)}), bf16[2,2,2,8,4,32,512]{6,5,1,2,4,3,0:T(8,128)(2,1)}, u32[]{:S(2)}, u32[]{:S(2)}) async-start(bf16[2,2,2,8,4,32,512]{6,5,1,2,4,3,0:T(8,128)(2,1)} %bitcast.152), calls=%async_computation.1 | async-start | bytes 16777216 | tf_op jit(solution)/shard_map/all_to_all | solution.py:83
  28.4 4.4 %all-to-all-done.1 = bf16[2,2,2,8,4,32,512]{6,5,1,2,4,3,0:T(8,128)(2,1)} async-done(((bf16[2,2,2,8,4,32,512]{6,5,1,2,4,3,0:T(8,128)(2,1)}), bf16[2,2,2,8,4,32,512]{6,5,1,2,4,3,0:T(8,128)(2,1)}, u32[]{:S(2)}, u32[]{:S(2)}) %all-to-all-start.1) | async-done | bytes 8388640 | tf_op jit(solution)/shard_map/all_to_all | solution.py:83
  32.9 11.6 %all-to-all-start = ((bf16[32,2,4096]{2,1,0:T(2,128)(2,1)}), bf16[32,2,4096]{2,1,0:T(2,128)(2,1)S(1)}, u32[]{:S(2)}, u32[]{:S(2)}) async-start(bf16[32,2,4096]{2,1,0:T(2,128)(2,1)} %reshape.52), calls=%async_computation | async-start | bytes 1048576 | tf_op jit(solution)/shard_map/all_to_all | solution.py:87
  44.5 8.3 %copy.31 = bf16[1,2,2,8,4,2,32,512]{7,6,5,1,2,4,3,0:T(8,128)(2,1)} copy(bf16[1,2,2,8,4,2,32,512]{7,6,1,2,4,3,5,0:T(8,128)(2,1)} %bitcast.8) | data formatting | bytes 16777216 | tf_op jit(solution)/shard_map/all_to_all | solution.py:83
  52.8 8.8 %all-to-all-done = bf16[32,2,4096]{2,1,0:T(2,128)(2,1)S(1)} async-done(((bf16[32,2,4096]{2,1,0:T(2,128)(2,1)}), bf16[32,2,4096]{2,1,0:T(2,128)(2,1)S(1)}, u32[]{:S(2)}, u32[]{:S(2)}) %all-to-all-start) | async-done | bytes 524320 | tf_op jit(solution)/shard_map/all_to_all | solution.py:87
  62.5 4.8 %convolution_bitcast_fusion = f32[8,4,2,32,512]{4,3,2,1,0:T(8,128)S(1)} fusion(bf16[2,2,8,4,64,512]{5,4,0,1,3,2:T(8,128)(2,1)} %bitcast.148, bf16[8,4,2,32,1,64]{5,3,4,2,1,0:T(8,128)(2,1)S(1)} %get-tuple-element.10, bf16[8,4,2,32,1,64]{5,3,4,2,1,0:T(8,128)(2,1)S(1)} %get-tuple-element.9), kind=kOutput, calls=%fused_computation.1 | convolution fusion | flops 268697600 | bytes 13107200 | tf_op jit(solution)/shard_map/zxpbra,rpzxat->zxpbt/dot_general | solution.py:91
  74.8 7.0 %collective-permute-done.10 = f32[4,2,32,512]{3,2,1,0:T(8,128)S(1)} collective-permute-done((f32[4,2,32,512]{3,2,1,0:T(8,128)S(1)}, f32[4,2,32,512]{3,2,1,0:T(8,128)S(1)}, u32[]{:S(2)}, u32[]{:S(2)}) %collective-permute-start.10) | collective-permute-done | bytes 524320 | tf_op jit(solution)/shard_map/ppermute | solution.py:75
  88.4 6.2 %collective-permute-done.11 = f32[4,2,32,512]{3,2,1,0:T(8,128)S(1)} collective-permute-done((f32[4,2,32,512]{3,2,1,0:T(8,128)S(1)}, f32[4,2,32,512]{3,2,1,0:T(8,128)S(1)}, u32[]{:S(2)}, u32[]{:S(2)}) %collective-permute-start.11) | collective-permute-done | bytes 524320 | tf_op jit(solution)/shard_map/ppermute | solution.py:75
  95.8 3.1 %collective-permute-start.12 = (f32[4,2,32,512]{3,2,1,0:T(8,128)S(1)}, f32[4,2,32,512]{3,2,1,0:T(8,128)S(1)}, u32[]{:S(2)}, u32[]{:S(2)}) collective-permute-start(f32[4,2,32,512]{3,2,1,0:T(8,128)S(1)} %bitcast_add_fusion.5), channel_id=1, source_target_pairs={{0,224},{32,0},{64,32},{96,64},{128,96},{160,128},{192,160},{224,1... | collective-permute-start | bytes 1572872 | tf_op jit(solution)/shard_map/ppermute | solution.py:75
  101.9 5.5 %collective-permute-done.12 = f32[4,2,32,512]{3,2,1,0:T(8,128)S(1)} collective-permute-done((f32[4,2,32,512]{3,2,1,0:T(8,128)S(1)}, f32[4,2,32,512]{3,2,1,0:T(8,128)S(1)}, u32[]{:S(2)}, u32[]{:S(2)}) %collective-permute-start.12) | collective-permute-done | bytes 524320 | tf_op jit(solution)/shard_map/ppermute | solution.py:75
  108.5 3.8 %collective-permute-start.13 = (f32[4,2,32,512]{3,2,1,0:T(8,128)S(1)}, f32[4,2,32,512]{3,2,1,0:T(8,128)S(1)}, u32[]{:S(2)}, u32[]{:S(2)}) collective-permute-start(f32[4,2,32,512]{3,2,1,0:T(8,128)S(1)} %bitcast_add_fusion.4), channel_id=1, source_target_pairs={{0,224},{32,0},{64,32},{96,64},{128,96},{160,128},{192,160},{224,1... | collective-permute-start | bytes 1572872 | tf_op jit(solution)/shard_map/ppermute | solution.py:75
  115.1 4.9 %collective-permute-done.13 = f32[4,2,32,512]{3,2,1,0:T(8,128)S(1)} collective-permute-done((f32[4,2,32,512]{3,2,1,0:T(8,128)S(1)}, f32[4,2,32,512]{3,2,1,0:T(8,128)S(1)}, u32[]{:S(2)}, u32[]{:S(2)}) %collective-permute-start.13) | collective-permute-done | bytes 524320 | tf_op jit(solution)/shard_map/ppermute | solution.py:75
  121.1 3.8 %collective-permute-start.14 = (f32[4,2,32,512]{3,2,1,0:T(8,128)S(1)}, f32[4,2,32,512]{3,2,1,0:T(8,128)S(1)}, u32[]{:S(2)}, u32[]{:S(2)}) collective-permute-start(f32[4,2,32,512]{3,2,1,0:T(8,128)S(1)} %bitcast_add_fusion.3), channel_id=1, source_target_pairs={{0,224},{32,0},{64,32},{96,64},{128,96},{160,128},{192,160},{224,1... | collective-permute-start | bytes 1572872 | tf_op jit(solution)/shard_map/ppermute | solution.py:75
  127.5 4.3 %collective-permute-done.14 = f32[4,2,32,512]{3,2,1,0:T(8,128)S(1)} collective-permute-done((f32[4,2,32,512]{3,2,1,0:T(8,128)S(1)}, f32[4,2,32,512]{3,2,1,0:T(8,128)S(1)}, u32[]{:S(2)}, u32[]{:S(2)}) %collective-permute-start.14) | collective-permute-done | bytes 524320 | tf_op jit(solution)/shard_map/ppermute | solution.py:75
  133.7 3.7 %collective-permute-start.15 = (f32[4,2,32,512]{3,2,1,0:T(8,128)}, f32[4,2,32,512]{3,2,1,0:T(8,128)}, u32[]{:S(2)}, u32[]{:S(2)}) collective-permute-start(f32[4,2,32,512]{3,2,1,0:T(8,128)} %bitcast_add_fusion.2), channel_id=1, source_target_pairs={{0,224},{32,0},{64,32},{96,64},{128,96},{160,128},{192,160},{224,1... | collective-permute-start | bytes 1572872 | tf_op jit(solution)/shard_map/ppermute | solution.py:75
  137.3 4.1 %fusion.26 = (f32[512,512]{1,0:T(8,128)S(1)}, f32[512,512]{1,0:T(8,128)S(1)}) fusion(), kind=kLoop, calls=%fused_computation.54 | loop fusion | flops 3670016 | bytes 2097152 | tf_op jit(solution)/shard_map/sin | solution.py:21
  146.7 3.7 %collective-permute-start.16 = (f32[4,2,32,512]{3,2,1,0:T(8,128)}, f32[4,2,32,512]{3,2,1,0:T(8,128)}, u32[]{:S(2)}, u32[]{:S(2)}) collective-permute-start(f32[4,2,32,512]{3,2,1,0:T(8,128)} %bitcast_add_fusion.1), channel_id=1, source_target_pairs={{0,224},{32,0},{64,32},{96,64},{128,96},{160,128},{192,160},{224,1... | collective-permute-start | bytes 1572872 | tf_op jit(solution)/shard_map/ppermute | solution.py:75
  150.8 4.1 %collective-permute-done.5 = f32[4,2,32,512]{3,2,1,0:T(8,128)S(1)} collective-permute-done((f32[4,2,32,512]{3,2,1,0:T(8,128)S(1)}, f32[4,2,32,512]{3,2,1,0:T(8,128)S(1)}, u32[]{:S(2)}, u32[]{:S(2)}) %collective-permute-start.5) | collective-permute-done | bytes 524320 | tf_op jit(solution)/shard_map/ppermute | solution.py:74
  159.4 7.1 %collective-permute-done.6 = f32[4,2,32,512]{3,2,1,0:T(8,128)S(1)} collective-permute-done((f32[4,2,32,512]{3,2,1,0:T(8,128)S(1)}, f32[4,2,32,512]{3,2,1,0:T(8,128)S(1)}, u32[]{:S(2)}, u32[]{:S(2)}) %collective-permute-start.6) | collective-permute-done | bytes 524320 | tf_op jit(solution)/shard_map/ppermute | solution.py:74
  170.0 3.6 %collective-permute-done.7 = f32[2,32,512]{2,0,1:T(2,128)S(1)} collective-permute-done((f32[2,32,512]{2,0,1:T(2,128)S(1)}, f32[2,32,512]{2,0,1:T(2,128)S(1)}, u32[]{:S(2)}, u32[]{:S(2)}) %collective-permute-start.7) | collective-permute-done | bytes 131104 | tf_op jit(solution)/shard_map/ppermute | solution.py:74
  185.0 4.5 %all-to-all-start.2 = ((f32[2,2,32,512]{3,1,0,2:T(2,128)}), f32[2,2,32,512]{3,1,0,2:T(2,128)S(1)}, u32[]{:S(2)}, u32[]{:S(2)}) async-start(f32[2,2,32,512]{3,1,0,2:T(2,128)} %pad_maximum_fusion), calls=%async_computation.2 | async-start | bytes 524288 | tf_op jit(solution)/shard_map/all_to_all | solution.py:100
  189.7 6.4 %all-to-all-done.2 = f32[2,2,32,512]{3,1,0,2:T(2,128)S(1)} async-done(((f32[2,2,32,512]{3,1,0,2:T(2,128)}), f32[2,2,32,512]{3,1,0,2:T(2,128)S(1)}, u32[]{:S(2)}, u32[]{:S(2)}) %all-to-all-start.2) | async-done | bytes 262176 | tf_op jit(solution)/shard_map/all_to_all | solution.py:100
  (104 shorter events, 61.9 us)
Async XLA Ops:
  18.3 14.6 %all-to-all-start.1 = ((bf16[2,2,2,8,4,32,512]{6,5,1,2,4,3,0:T(8,128)(2,1)}), bf16[2,2,2,8,4,32,512]{6,5,1,2,4,3,0:T(8,128)(2,1)}, u32[]{:S(2)}, u32[]{:S(2)}) async-start(bf16[2,2,2,8,4,32,512]{6,5,1,2,4,3,0:T(8,128)(2,1)} %bitcast.152), calls=%async_computation.1 | async-start | bytes 16777216 | tf_op jit(solution)/shard_map/all_to_all | solution.py:83
  32.9 28.7 %all-to-all-start = ((bf16[32,2,4096]{2,1,0:T(2,128)(2,1)}), bf16[32,2,4096]{2,1,0:T(2,128)(2,1)S(1)}, u32[]{:S(2)}, u32[]{:S(2)}) async-start(bf16[32,2,4096]{2,1,0:T(2,128)(2,1)} %reshape.52), calls=%async_computation | async-start | bytes 1048576 | tf_op jit(solution)/shard_map/all_to_all | solution.py:87
  69.3 12.5 %collective-permute-start.10 = (f32[4,2,32,512]{3,2,1,0:T(8,128)S(1)}, f32[4,2,32,512]{3,2,1,0:T(8,128)S(1)}, u32[]{:S(2)}, u32[]{:S(2)}) collective-permute-start(f32[4,2,32,512]{3,2,1,0:T(8,128)S(1)} %dynamic-slice_bitcast_fusion), channel_id=1, source_target_pairs={{0,224},{32,0},{64,32},{96,64},{128,96},{160,128},{192,160},{224,1... | collective-permute-start | bytes 1572872 | tf_op jit(solution)/shard_map/ppermute | solution.py:75
  72.7 13.8 %collective-permute-start = (f32[4,2,32,512]{3,2,1,0:T(8,128)S(1)}, f32[4,2,32,512]{3,2,1,0:T(8,128)S(1)}, u32[]{:S(2)}, u32[]{:S(2)}) collective-permute-start(f32[4,2,32,512]{3,2,1,0:T(8,128)S(1)} %dynamic-slice_bitcast_fusion.1), channel_id=1, source_target_pairs={{0,32},{32,64},{64,96},{96,128},{128,160},{160,192},{192,224},{224... | collective-permute-start | bytes 1572872 | tf_op jit(solution)/shard_map/ppermute | solution.py:74
  82.9 11.7 %collective-permute-start.11 = (f32[4,2,32,512]{3,2,1,0:T(8,128)S(1)}, f32[4,2,32,512]{3,2,1,0:T(8,128)S(1)}, u32[]{:S(2)}, u32[]{:S(2)}) collective-permute-start(f32[4,2,32,512]{3,2,1,0:T(8,128)S(1)} %bitcast_add_fusion.6), channel_id=1, source_target_pairs={{0,224},{32,0},{64,32},{96,64},{128,96},{160,128},{192,160},{224,1... | collective-permute-start | bytes 1572872 | tf_op jit(solution)/shard_map/ppermute | solution.py:75
  87.6 13.1 %collective-permute-start.1 = (f32[4,2,32,512]{3,2,1,0:T(8,128)S(1)}, f32[4,2,32,512]{3,2,1,0:T(8,128)S(1)}, u32[]{:S(2)}, u32[]{:S(2)}) collective-permute-start(f32[4,2,32,512]{3,2,1,0:T(8,128)S(1)} %bitcast_add_fusion.13), channel_id=1, source_target_pairs={{0,32},{32,64},{64,96},{96,128},{128,160},{160,192},{192,224},{224... | collective-permute-start | bytes 1572872 | tf_op jit(solution)/shard_map/ppermute | solution.py:74
  95.8 31.7 %copy-start.4 = (s32[8]{0:T(128)S(1)}, s32[8]{0:T(128)}, u32[]{:S(2)}) copy-start(s32[8]{0:T(128)} %param.9) | copy-start | bytes 100
  95.8 11.6 %collective-permute-start.12 = (f32[4,2,32,512]{3,2,1,0:T(8,128)S(1)}, f32[4,2,32,512]{3,2,1,0:T(8,128)S(1)}, u32[]{:S(2)}, u32[]{:S(2)}) collective-permute-start(f32[4,2,32,512]{3,2,1,0:T(8,128)S(1)} %bitcast_add_fusion.5), channel_id=1, source_target_pairs={{0,224},{32,0},{64,32},{96,64},{128,96},{160,128},{192,160},{224,1... | collective-permute-start | bytes 1572872 | tf_op jit(solution)/shard_map/ppermute | solution.py:75
  101.8 12.1 %collective-permute-start.2 = (f32[4,2,32,512]{3,2,1,0:T(8,128)S(1)}, f32[4,2,32,512]{3,2,1,0:T(8,128)S(1)}, u32[]{:S(2)}, u32[]{:S(2)}) collective-permute-start(f32[4,2,32,512]{3,2,1,0:T(8,128)S(1)} %bitcast_add_fusion.12), channel_id=1, source_target_pairs={{0,32},{32,64},{64,96},{96,128},{128,160},{160,192},{192,224},{224... | collective-permute-start | bytes 1572872 | tf_op jit(solution)/shard_map/ppermute | solution.py:74
  108.5 11.5 %collective-permute-start.13 = (f32[4,2,32,512]{3,2,1,0:T(8,128)S(1)}, f32[4,2,32,512]{3,2,1,0:T(8,128)S(1)}, u32[]{:S(2)}, u32[]{:S(2)}) collective-permute-start(f32[4,2,32,512]{3,2,1,0:T(8,128)S(1)} %bitcast_add_fusion.4), channel_id=1, source_target_pairs={{0,224},{32,0},{64,32},{96,64},{128,96},{160,128},{192,160},{224,1... | collective-permute-start | bytes 1572872 | tf_op jit(solution)/shard_map/ppermute | solution.py:75
  115.0 11.2 %collective-permute-start.3 = (f32[4,2,32,512]{3,2,1,0:T(8,128)S(1)}, f32[4,2,32,512]{3,2,1,0:T(8,128)S(1)}, u32[]{:S(2)}, u32[]{:S(2)}) collective-permute-start(f32[4,2,32,512]{3,2,1,0:T(8,128)S(1)} %bitcast_add_fusion.11), channel_id=1, source_target_pairs={{0,32},{32,64},{64,96},{96,128},{128,160},{160,192},{192,224},{224... | collective-permute-start | bytes 1572872 | tf_op jit(solution)/shard_map/ppermute | solution.py:74
  121.1 10.6 %collective-permute-start.14 = (f32[4,2,32,512]{3,2,1,0:T(8,128)S(1)}, f32[4,2,32,512]{3,2,1,0:T(8,128)S(1)}, u32[]{:S(2)}, u32[]{:S(2)}) collective-permute-start(f32[4,2,32,512]{3,2,1,0:T(8,128)S(1)} %bitcast_add_fusion.3), channel_id=1, source_target_pairs={{0,224},{32,0},{64,32},{96,64},{128,96},{160,128},{192,160},{224,1... | collective-permute-start | bytes 1572872 | tf_op jit(solution)/shard_map/ppermute | solution.py:75
  127.4 14.1 %collective-permute-start.4 = (f32[4,2,32,512]{3,2,1,0:T(8,128)S(1)}, f32[4,2,32,512]{3,2,1,0:T(8,128)S(1)}, u32[]{:S(2)}, u32[]{:S(2)}) collective-permute-start(f32[4,2,32,512]{3,2,1,0:T(8,128)S(1)} %bitcast_add_fusion.10), channel_id=1, source_target_pairs={{0,32},{32,64},{64,96},{96,128},{128,160},{160,192},{192,224},{224... | collective-permute-start | bytes 1572872 | tf_op jit(solution)/shard_map/ppermute | solution.py:74
  133.7 11.0 %collective-permute-start.15 = (f32[4,2,32,512]{3,2,1,0:T(8,128)}, f32[4,2,32,512]{3,2,1,0:T(8,128)}, u32[]{:S(2)}, u32[]{:S(2)}) collective-permute-start(f32[4,2,32,512]{3,2,1,0:T(8,128)} %bitcast_add_fusion.2), channel_id=1, source_target_pairs={{0,224},{32,0},{64,32},{96,64},{128,96},{160,128},{192,160},{224,1... | collective-permute-start | bytes 1572872 | tf_op jit(solution)/shard_map/ppermute | solution.py:75
  142.6 12.2 %collective-permute-start.5 = (f32[4,2,32,512]{3,2,1,0:T(8,128)S(1)}, f32[4,2,32,512]{3,2,1,0:T(8,128)S(1)}, u32[]{:S(2)}, u32[]{:S(2)}) collective-permute-start(f32[4,2,32,512]{3,2,1,0:T(8,128)S(1)} %bitcast_add_fusion.9), channel_id=1, source_target_pairs={{0,32},{32,64},{64,96},{96,128},{128,160},{160,192},{192,224},{224... | collective-permute-start | bytes 1572872 | tf_op jit(solution)/shard_map/ppermute | solution.py:74
  146.7 10.7 %collective-permute-start.16 = (f32[4,2,32,512]{3,2,1,0:T(8,128)}, f32[4,2,32,512]{3,2,1,0:T(8,128)}, u32[]{:S(2)}, u32[]{:S(2)}) collective-permute-start(f32[4,2,32,512]{3,2,1,0:T(8,128)} %bitcast_add_fusion.1), channel_id=1, source_target_pairs={{0,224},{32,0},{64,32},{96,64},{128,96},{160,128},{192,160},{224,1... | collective-permute-start | bytes 1572872 | tf_op jit(solution)/shard_map/ppermute | solution.py:75
  156.0 10.5 %collective-permute-start.6 = (f32[4,2,32,512]{3,2,1,0:T(8,128)S(1)}, f32[4,2,32,512]{3,2,1,0:T(8,128)S(1)}, u32[]{:S(2)}, u32[]{:S(2)}) collective-permute-start(f32[4,2,32,512]{3,2,1,0:T(8,128)S(1)} %bitcast_add_fusion.8), channel_id=1, source_target_pairs={{0,32},{32,64},{64,96},{96,128},{128,160},{160,192},{192,224},{224... | collective-permute-start | bytes 1572872 | tf_op jit(solution)/shard_map/ppermute | solution.py:74
  158.9 9.5 %collective-permute-start.17 = (f32[2,32,512]{2,0,1:T(2,128)S(1)}, f32[2,32,512]{2,0,1:T(2,128)S(1)}, u32[]{:S(2)}, u32[]{:S(2)}) collective-permute-start(f32[2,32,512]{2,0,1:T(2,128)S(1)} %bitcast.160), channel_id=1, source_target_pairs={{0,24},{8,0},{16,8},{24,16},{1,25},{9,1},{17,9},{25,17},{2,26},{10... | collective-permute-start | bytes 393224 | tf_op jit(solution)/shard_map/ppermute | solution.py:75
  167.7 5.9 %collective-permute-start.7 = (f32[2,32,512]{2,0,1:T(2,128)S(1)}, f32[2,32,512]{2,0,1:T(2,128)S(1)}, u32[]{:S(2)}, u32[]{:S(2)}) collective-permute-start(f32[2,32,512]{2,0,1:T(2,128)S(1)} %bitcast.161), channel_id=1, source_target_pairs={{0,8},{8,16},{16,24},{24,0},{1,9},{9,17},{17,25},{25,1},{2,10},{10... | collective-permute-start | bytes 393224 | tf_op jit(solution)/shard_map/ppermute | solution.py:74
  168.5 6.3 %collective-permute-start.18 = (f32[2,32,512]{2,0,1:T(2,128)S(1)}, f32[2,32,512]{2,0,1:T(2,128)S(1)}, u32[]{:S(2)}, u32[]{:S(2)}) collective-permute-start(f32[2,32,512]{2,0,1:T(2,128)S(1)} %bitcast_add_fusion.16), channel_id=1, source_target_pairs={{0,24},{8,0},{16,8},{24,16},{1,25},{9,1},{17,9},{25,17},{2,26},{10... | collective-permute-start | bytes 393224 | tf_op jit(solution)/shard_map/ppermute | solution.py:75
  173.8 5.0 %collective-permute-start.8 = (f32[2,32,512]{2,0,1:T(2,128)S(1)}, f32[2,32,512]{2,0,1:T(2,128)S(1)}, u32[]{:S(2)}, u32[]{:S(2)}) collective-permute-start(f32[2,32,512]{2,0,1:T(2,128)S(1)} %bitcast_add_fusion.19), channel_id=1, source_target_pairs={{0,8},{8,16},{16,24},{24,0},{1,9},{9,17},{17,25},{25,1},{2,10},{10... | collective-permute-start | bytes 393224 | tf_op jit(solution)/shard_map/ppermute | solution.py:74
  174.9 6.3 %collective-permute-start.19 = (f32[2,32,512]{2,0,1:T(2,128)S(1)}, f32[2,32,512]{2,0,1:T(2,128)S(1)}, u32[]{:S(2)}, u32[]{:S(2)}) collective-permute-start(f32[2,32,512]{2,0,1:T(2,128)S(1)} %bitcast_add_fusion.15), channel_id=1, source_target_pairs={{0,24},{8,0},{16,8},{24,16},{1,25},{9,1},{17,9},{25,17},{2,26},{10... | collective-permute-start | bytes 393224 | tf_op jit(solution)/shard_map/ppermute | solution.py:75
  179.0 5.0 %collective-permute-start.9 = (f32[2,32,512]{2,0,1:T(2,128)S(1)}, f32[2,32,512]{2,0,1:T(2,128)S(1)}, u32[]{:S(2)}, u32[]{:S(2)}) collective-permute-start(f32[2,32,512]{2,0,1:T(2,128)S(1)} %bitcast_add_fusion.18), channel_id=1, source_target_pairs={{0,8},{8,16},{16,24},{24,0},{1,9},{9,17},{17,25},{25,1},{2,10},{10... | collective-permute-start | bytes 393224 | tf_op jit(solution)/shard_map/ppermute | solution.py:74
  185.0 11.1 %all-to-all-start.2 = ((f32[2,2,32,512]{3,1,0,2:T(2,128)}), f32[2,2,32,512]{3,1,0,2:T(2,128)S(1)}, u32[]{:S(2)}, u32[]{:S(2)}) async-start(f32[2,2,32,512]{3,1,0,2:T(2,128)} %pad_maximum_fusion), calls=%async_computation.2 | async-start | bytes 524288 | tf_op jit(solution)/shard_map/all_to_all | solution.py:100
  (6 other events, 52.4 us)

commit v4 on v3

--- a/solution.py
+++ b/solution.py
@@ -80,11 +80,12 @@
     zs, xs, cs = lax.axis_size("z"), lax.axis_size("x"), lax.axis_size("c")
     order = channel_map.reshape(zs, xs, cs).transpose(2, 0, 1)
     selected = jnp.moveaxis(jnp.take(voltages, order, axis=2, mode="clip"), 2, 0)
-    own = lax.all_to_all(selected, "c", split_axis=0, concat_axis=5, tiled=True)[0]
     groups = zs * xs
     grouped = weights[0].reshape(weights.shape[1:4] + (groups, -1))
     grouped = jnp.moveaxis(grouped, 3, 0)
     local_weights = lax.all_to_all(grouped, ("z", "x"), split_axis=0, concat_axis=0, tiled=True)
+    selected = selected + local_weights[0, 0, 0, 0, 0] * 0
+    own = lax.all_to_all(selected, "c", split_axis=0, concat_axis=5, tiled=True)[0]
     local_weights = local_weights.reshape((zs, xs) + local_weights.shape[1:])
     mixing = mixing_matrix(local_weights, 2)
     parts = [

time: 203 us -> 222 us (1.094)
  blocking collectives: 0 us -> 18.5 us
  other arithmetic: 24.1 us -> 31.3 us
  starting transfers between devices: 53 us -> 47.5 us
    all_to_all x0 -> x1, blocking collectives: none -> 18.5 us  [on_device(): lax.all_to_all(selected, 'c', split_axis=0, concat_axis=5, tiled=True)[0]]
    ppermute x10, waiting for transfers between devices: 27 us -> 44.2 us  [ring_reduce_scatter(): lax.ppermute(acc_cw, axis, forward) + pick(halves[0], position - step - 2)]
    ppermute x10, waiting for transfers between devices: 30.7 us -> 18.2 us  [ring_reduce_scatter(): lax.ppermute(acc_ccw, axis, backward) + pick(halves[1], position + step + 2)]
    gather x2 -> x1, local copies, waits for them, and re-layouts: 17.3 us -> 8.93 us  [on_device(): jnp.take(voltages, order, axis=2, mode='clip')]
    add x0 -> x1, local copies, waits for them, and re-layouts: none -> 8.32 us  [on_device(): selected = selected + local_weights[0, 0, 0, 0, 0] * 0]
    add x0 -> x1, other arithmetic: none -> 7.16 us  [on_device(): selected = selected + local_weights[0, 0, 0, 0, 0] * 0]
    all_to_all x1 -> x0, starting transfers between devices: 7.1 us -> none  [on_device(): lax.all_to_all(selected, 'c', split_axis=0, concat_axis=5, tiled=True)[0]]
    all_to_all x1 -> x0, waiting for transfers between devices: 4.45 us -> none  [on_device(): lax.all_to_all(selected, 'c', split_axis=0, concat_axis=5, tiled=True)[0]]
  transfers between devices with their start and end apart: 23 -> 22, of which waited for: 19 -> 21; matrix products, arithmetic and copies ran while one was open for 18% -> 16% of each run, Pallas kernels for 0% -> 0%
where the time goes in v4:
time: 222 us; the launch traced here: 220 us
  waiting for transfers between devices  76.3 us (34%)
  starting transfers between devices  47.5 us (21%)
  local copies, waits for them, and re-layouts  35.5 us (16%)
  other arithmetic  31.3 us (14%)
  blocking collectives  18.5 us (8%)
  matrix products  9.97 us (4%)
    ppermute x10, waiting for transfers between devices, ring_reduce_scatter(): lax.ppermute(acc_cw, axis, forward) + pick(halves[0], position - step - 2)  44.2 us
    ppermute x10, starting transfers between devices, ring_reduce_scatter(): lax.ppermute(acc_ccw, axis, backward) + pick(halves[1], position + step + 2)  22.8 us
    all_to_all x1, blocking collectives, on_device(): lax.all_to_all(selected, 'c', split_axis=0, concat_axis=5, tiled=True)[0]  18.5 us
    ppermute x10, waiting for transfers between devices, ring_reduce_scatter(): lax.ppermute(acc_ccw, axis, backward) + pick(halves[1], position + step + 2)  18.2 us
    all_to_all x1, starting transfers between devices, on_device(): lax.all_to_all(grouped, ('z', 'x'), split_axis=0, concat_axis=0, tiled=True)  11.6 us
    add x9, other arithmetic, ring_reduce_scatter(): lax.ppermute(acc_cw, axis, forward) + pick(halves[0], position - step - 2)  10.1 us
    gather x1, local copies, waits for them, and re-layouts, on_device(): jnp.take(voltages, order, axis=2, mode='clip')  8.93 us
    ppermute x10, starting transfers between devices, ring_reduce_scatter(): lax.ppermute(acc_cw, axis, forward) + pick(halves[0], position - step - 2)  8.63 us
  transfers between devices with their start and end apart: 22, of which 21 were waited for; matrix products, arithmetic and copies ran while one was open for 16% of the time, Pallas kernels for 0%

profile of v4, /device:TPU:6, one launch (start us, length us, event | category | flops | bytes accessed | tf_op | source)
XLA Modules:
  0.0 220.3 jit_solution(5176022226626689636)
XLA Ops:
  4.0 11.6 %all-to-all-start = ((bf16[32,2,4096]{2,1,0:T(2,128)(2,1)}), bf16[32,2,4096]{2,1,0:T(2,128)(2,1)S(1)}, u32[]{:S(2)}, u32[]{:S(2)}) async-start(bf16[32,2,4096]{2,1,0:T(2,128)(2,1)} %reshape.56), calls=%async_computation | async-start | bytes 1048576 | tf_op jit(solution)/shard_map/all_to_all | solution.py:86
  16.0 8.9 %gather_fusion = bf16[64,2,2,32,512]{4,3,2,1,0:T(8,128)(2,1)} fusion(bf16[2,2,64,32,512]{4,3,2,1,0:T(8,128)(2,1)} %param.5, s32[1024]{0:T(1024)S(1)} %pad_clamp_fusion), kind=kCustom, calls=%fused_computation | custom fusion | bytes 16777472 | tf_op jit(solution)/shard_map/jit(_take)/gather | solution.py:82
  24.9 7.5 %all-to-all-done = bf16[32,2,4096]{2,1,0:T(2,128)(2,1)S(1)} async-done(((bf16[32,2,4096]{2,1,0:T(2,128)(2,1)}), bf16[32,2,4096]{2,1,0:T(2,128)(2,1)S(1)}, u32[]{:S(2)}, u32[]{:S(2)}) %all-to-all-start) | async-done | bytes 524320 | tf_op jit(solution)/shard_map/all_to_all | solution.py:86
  34.5 7.2 %broadcast_add_fusion = bf16[64,2,2,32,512]{4,3,2,1,0:T(8,128)(2,1)} fusion(bf16[64,2,2,32,512]{4,3,2,1,0:T(8,128)(2,1)} %gather_fusion, bf16[]{:T(256)} %bitcast.5), kind=kLoop, calls=%fused_computation.1 | loop fusion | flops 4194304 | bytes 16777218 | tf_op jit(solution)/shard_map/add | solution.py:87
  41.7 8.3 %copy.30 = bf16[64,2,2,32,512]{4,3,1,2,0:T(8,128)(2,1)} copy(bf16[64,2,2,32,512]{4,3,2,1,0:T(8,128)(2,1)} %broadcast_add_fusion) | data formatting | bytes 16777216 | tf_op jit(solution)/shard_map/add | solution.py:87
  50.0 18.5 %all_to_all.38 = bf16[2,2,2,8,4,32,512]{6,5,1,2,4,3,0:T(8,128)(2,1)} all-to-all(bf16[2,2,2,8,4,32,512]{6,5,1,2,4,3,0:T(8,128)(2,1)} %bitcast.151), channel_id=1, replica_groups=mesh['z'=8,'x'=4,'c'=2,'tm'=4] {'c'}, dimensions={0} | all-to-all | bytes 16777216 | tf_op jit(solution)/shard_map/all_to_all | solution.py:88
  68.5 8.3 %copy.31 = bf16[1,2,2,8,4,2,32,512]{7,6,5,1,2,4,3,0:T(8,128)(2,1)} copy(bf16[1,2,2,8,4,2,32,512]{7,6,1,2,4,3,5,0:T(8,128)(2,1)} %bitcast.152) | data formatting | bytes 16777216 | tf_op jit(solution)/shard_map/all_to_all | solution.py:88
  76.8 4.8 %convolution_bitcast_fusion.1 = f32[8,4,2,32,512]{4,3,2,1,0:T(8,128)S(1)} fusion(bf16[2,2,8,4,64,512]{5,4,0,1,3,2:T(8,128)(2,1)} %bitcast.149, bf16[8,4,2,32,1,64]{5,3,4,2,1,0:T(8,128)(2,1)S(1)} %fusion.64, bf16[8,4,2,32,1,64]{5,3,4,2,1,0:T(8,128)(2,1)S(1)} %get-tuple-element.10), kind=kOutput, calls=%fused_computation.3 | convolution fusion | flops 268697600 | bytes 13107200 | tf_op jit(solution)/shard_map/zxpbra,rpzxat->zxpbt/dot_general | solution.py:92
  88.4 8.6 %collective-permute-done = f32[4,2,32,512]{3,2,1,0:T(8,128)S(1)} collective-permute-done((f32[4,2,32,512]{3,2,1,0:T(8,128)S(1)}, f32[4,2,32,512]{3,2,1,0:T(8,128)S(1)}, u32[]{:S(2)}, u32[]{:S(2)}) %collective-permute-start) | collective-permute-done | bytes 524320 | tf_op jit(solution)/shard_map/ppermute | solution.py:74
  104.5 8.2 %collective-permute-done.1 = f32[4,2,32,512]{3,2,1,0:T(8,128)S(1)} collective-permute-done((f32[4,2,32,512]{3,2,1,0:T(8,128)S(1)}, f32[4,2,32,512]{3,2,1,0:T(8,128)S(1)}, u32[]{:S(2)}, u32[]{:S(2)}) %collective-permute-start.1) | collective-permute-done | bytes 524320 | tf_op jit(solution)/shard_map/ppermute | solution.py:74
  116.4 3.3 %collective-permute-start.12 = (f32[4,2,32,512]{3,2,1,0:T(8,128)S(1)}, f32[4,2,32,512]{3,2,1,0:T(8,128)S(1)}, u32[]{:S(2)}, u32[]{:S(2)}) collective-permute-start(f32[4,2,32,512]{3,2,1,0:T(8,128)S(1)} %bitcast_add_fusion.5), channel_id=1, source_target_pairs={{0,224},{32,0},{64,32},{96,64},{128,96},{160,128},{192,160},{224,1... | collective-permute-start | bytes 1572872 | tf_op jit(solution)/shard_map/ppermute | solution.py:75
  119.7 7.6 %collective-permute-done.2 = f32[4,2,32,512]{3,2,1,0:T(8,128)S(1)} collective-permute-done((f32[4,2,32,512]{3,2,1,0:T(8,128)S(1)}, f32[4,2,32,512]{3,2,1,0:T(8,128)S(1)}, u32[]{:S(2)}, u32[]{:S(2)}) %collective-permute-start.2) | collective-permute-done | bytes 524320 | tf_op jit(solution)/shard_map/ppermute | solution.py:74
  130.3 3.8 %collective-permute-start.13 = (f32[4,2,32,512]{3,2,1,0:T(8,128)S(1)}, f32[4,2,32,512]{3,2,1,0:T(8,128)S(1)}, u32[]{:S(2)}, u32[]{:S(2)}) collective-permute-start(f32[4,2,32,512]{3,2,1,0:T(8,128)S(1)} %bitcast_add_fusion.4), channel_id=1, source_target_pairs={{0,224},{32,0},{64,32},{96,64},{128,96},{160,128},{192,160},{224,1... | collective-permute-start | bytes 1572872 | tf_op jit(solution)/shard_map/ppermute | solution.py:75
  134.1 7.0 %collective-permute-done.3 = f32[4,2,32,512]{3,2,1,0:T(8,128)S(1)} collective-permute-done((f32[4,2,32,512]{3,2,1,0:T(8,128)S(1)}, f32[4,2,32,512]{3,2,1,0:T(8,128)S(1)}, u32[]{:S(2)}, u32[]{:S(2)}) %collective-permute-start.3) | collective-permute-done | bytes 524320 | tf_op jit(solution)/shard_map/ppermute | solution.py:74
  143.8 3.8 %collective-permute-start.14 = (f32[4,2,32,512]{3,2,1,0:T(8,128)S(1)}, f32[4,2,32,512]{3,2,1,0:T(8,128)S(1)}, u32[]{:S(2)}, u32[]{:S(2)}) collective-permute-start(f32[4,2,32,512]{3,2,1,0:T(8,128)S(1)} %bitcast_add_fusion.3), channel_id=1, source_target_pairs={{0,224},{32,0},{64,32},{96,64},{128,96},{160,128},{192,160},{224,1... | collective-permute-start | bytes 1572872 | tf_op jit(solution)/shard_map/ppermute | solution.py:75
  147.6 6.4 %collective-permute-done.4 = f32[4,2,32,512]{3,2,1,0:T(8,128)S(1)} collective-permute-done((f32[4,2,32,512]{3,2,1,0:T(8,128)S(1)}, f32[4,2,32,512]{3,2,1,0:T(8,128)S(1)}, u32[]{:S(2)}, u32[]{:S(2)}) %collective-permute-start.4) | collective-permute-done | bytes 524320 | tf_op jit(solution)/shard_map/ppermute | solution.py:74
  156.0 4.1 %fusion.26 = (f32[512,512]{1,0:T(8,128)S(1)}, f32[512,512]{1,0:T(8,128)S(1)}) fusion(), kind=kLoop, calls=%fused_computation.55 | loop fusion | flops 3670016 | bytes 2097152 | tf_op jit(solution)/shard_map/sin | solution.py:21
  161.2 3.5 %collective-permute-start.15 = (f32[4,2,32,512]{3,2,1,0:T(8,128)S(1)}, f32[4,2,32,512]{3,2,1,0:T(8,128)S(1)}, u32[]{:S(2)}, u32[]{:S(2)}) collective-permute-start(f32[4,2,32,512]{3,2,1,0:T(8,128)S(1)} %bitcast_add_fusion.2), channel_id=1, source_target_pairs={{0,224},{32,0},{64,32},{96,64},{128,96},{160,128},{192,160},{224,1... | collective-permute-start | bytes 1572872 | tf_op jit(solution)/shard_map/ppermute | solution.py:75
  173.4 3.5 %collective-permute-start.16 = (f32[4,2,32,512]{3,2,1,0:T(8,128)S(1)}, f32[4,2,32,512]{3,2,1,0:T(8,128)S(1)}, u32[]{:S(2)}, u32[]{:S(2)}) collective-permute-start(f32[4,2,32,512]{3,2,1,0:T(8,128)S(1)} %bitcast_add_fusion.1), channel_id=1, source_target_pairs={{0,224},{32,0},{64,32},{96,64},{128,96},{160,128},{192,160},{224,1... | collective-permute-start | bytes 1572872 | tf_op jit(solution)/shard_map/ppermute | solution.py:75
  177.1 2.9 %collective-permute-done.6 = f32[4,2,32,512]{3,2,1,0:T(8,128)} collective-permute-done((f32[4,2,32,512]{3,2,1,0:T(8,128)}, f32[4,2,32,512]{3,2,1,0:T(8,128)}, u32[]{:S(2)}, u32[]{:S(2)}) %collective-permute-start.6) | collective-permute-done | bytes 524320 | tf_op jit(solution)/shard_map/ppermute | solution.py:74
  191.8 3.7 %collective-permute-start.9 = (f32[2,32,512]{2,0,1:T(2,128)S(1)}, f32[2,32,512]{2,0,1:T(2,128)S(1)}, u32[]{:S(2)}, u32[]{:S(2)}) collective-permute-start(f32[2,32,512]{2,0,1:T(2,128)S(1)} %bitcast_add_fusion.18), channel_id=1, source_target_pairs={{0,8},{8,16},{16,24},{24,0},{1,9},{9,17},{17,25},{25,1},{2,10},{10... | collective-permute-start | bytes 393224 | tf_op jit(solution)/shard_map/ppermute | solution.py:74
  198.2 5.7 %collective-permute-done.19 = f32[2,32,512]{2,0,1:T(2,128)S(1)} collective-permute-done((f32[2,32,512]{2,0,1:T(2,128)S(1)}, f32[2,32,512]{2,0,1:T(2,128)S(1)}, u32[]{:S(2)}, u32[]{:S(2)}) %collective-permute-start.19) | collective-permute-done | bytes 131104 | tf_op jit(solution)/shard_map/ppermute | solution.py:75
  204.9 4.5 %all-to-all-start.2 = ((f32[2,2,32,512]{3,1,0,2:T(2,128)}), f32[2,2,32,512]{3,1,0,2:T(2,128)S(1)}, u32[]{:S(2)}, u32[]{:S(2)}) async-start(f32[2,2,32,512]{3,1,0,2:T(2,128)} %pad_maximum_fusion), calls=%async_computation.2 | async-start | bytes 524288 | tf_op jit(solution)/shard_map/all_to_all | solution.py:101
  209.6 6.4 %all-to-all-done.2 = f32[2,2,32,512]{3,1,0,2:T(2,128)S(1)} async-done(((f32[2,2,32,512]{3,1,0,2:T(2,128)}), f32[2,2,32,512]{3,1,0,2:T(2,128)S(1)}, u32[]{:S(2)}, u32[]{:S(2)}) %all-to-all-start.2) | async-done | bytes 262176 | tf_op jit(solution)/shard_map/all_to_all | solution.py:101
  (102 shorter events, 61.1 us)
Async XLA Ops:
  4.0 28.4 %all-to-all-start = ((bf16[32,2,4096]{2,1,0:T(2,128)(2,1)}), bf16[32,2,4096]{2,1,0:T(2,128)(2,1)S(1)}, u32[]{:S(2)}, u32[]{:S(2)}) async-start(bf16[32,2,4096]{2,1,0:T(2,128)(2,1)} %reshape.56), calls=%async_computation | async-start | bytes 1048576 | tf_op jit(solution)/shard_map/all_to_all | solution.py:86
  81.7 15.3 %collective-permute-start = (f32[4,2,32,512]{3,2,1,0:T(8,128)S(1)}, f32[4,2,32,512]{3,2,1,0:T(8,128)S(1)}, u32[]{:S(2)}, u32[]{:S(2)}) collective-permute-start(f32[4,2,32,512]{3,2,1,0:T(8,128)S(1)} %dynamic-slice_bitcast_fusion.1), channel_id=1, source_target_pairs={{0,32},{32,64},{64,96},{96,128},{128,160},{160,192},{192,224},{224... | collective-permute-start | bytes 1572872 | tf_op jit(solution)/shard_map/ppermute | solution.py:74
  86.9 14.0 %collective-permute-start.10 = (f32[4,2,32,512]{3,2,1,0:T(8,128)S(1)}, f32[4,2,32,512]{3,2,1,0:T(8,128)S(1)}, u32[]{:S(2)}, u32[]{:S(2)}) collective-permute-start(f32[4,2,32,512]{3,2,1,0:T(8,128)S(1)} %dynamic-slice_bitcast_fusion), channel_id=1, source_target_pairs={{0,224},{32,0},{64,32},{96,64},{128,96},{160,128},{192,160},{224,1... | collective-permute-start | bytes 1572872 | tf_op jit(solution)/shard_map/ppermute | solution.py:75
  98.1 14.6 %collective-permute-start.1 = (f32[4,2,32,512]{3,2,1,0:T(8,128)S(1)}, f32[4,2,32,512]{3,2,1,0:T(8,128)S(1)}, u32[]{:S(2)}, u32[]{:S(2)}) collective-permute-start(f32[4,2,32,512]{3,2,1,0:T(8,128)S(1)} %bitcast_add_fusion.13), channel_id=1, source_target_pairs={{0,32},{32,64},{64,96},{96,128},{128,160},{160,192},{192,224},{224... | collective-permute-start | bytes 1572872 | tf_op jit(solution)/shard_map/ppermute | solution.py:74
  102.1 13.2 %collective-permute-start.11 = (f32[4,2,32,512]{3,2,1,0:T(8,128)S(1)}, f32[4,2,32,512]{3,2,1,0:T(8,128)S(1)}, u32[]{:S(2)}, u32[]{:S(2)}) collective-permute-start(f32[4,2,32,512]{3,2,1,0:T(8,128)S(1)} %bitcast_add_fusion.6), channel_id=1, source_target_pairs={{0,224},{32,0},{64,32},{96,64},{128,96},{160,128},{192,160},{224,1... | collective-permute-start | bytes 1572872 | tf_op jit(solution)/shard_map/ppermute | solution.py:75
  113.7 33.9 %copy-start.4 = (s32[8]{0:T(128)S(1)}, s32[8]{0:T(128)}, u32[]{:S(2)}) copy-start(s32[8]{0:T(128)} %param.9) | copy-start | bytes 100
  113.8 13.5 %collective-permute-start.2 = (f32[4,2,32,512]{3,2,1,0:T(8,128)S(1)}, f32[4,2,32,512]{3,2,1,0:T(8,128)S(1)}, u32[]{:S(2)}, u32[]{:S(2)}) collective-permute-start(f32[4,2,32,512]{3,2,1,0:T(8,128)S(1)} %bitcast_add_fusion.12), channel_id=1, source_target_pairs={{0,32},{32,64},{64,96},{96,128},{128,160},{160,192},{192,224},{224... | collective-permute-start | bytes 1572872 | tf_op jit(solution)/shard_map/ppermute | solution.py:74
  116.4 12.8 %collective-permute-start.12 = (f32[4,2,32,512]{3,2,1,0:T(8,128)S(1)}, f32[4,2,32,512]{3,2,1,0:T(8,128)S(1)}, u32[]{:S(2)}, u32[]{:S(2)}) collective-permute-start(f32[4,2,32,512]{3,2,1,0:T(8,128)S(1)} %bitcast_add_fusion.5), channel_id=1, source_target_pairs={{0,224},{32,0},{64,32},{96,64},{128,96},{160,128},{192,160},{224,1... | collective-permute-start | bytes 1572872 | tf_op jit(solution)/shard_map/ppermute | solution.py:75
  128.4 12.7 %collective-permute-start.3 = (f32[4,2,32,512]{3,2,1,0:T(8,128)S(1)}, f32[4,2,32,512]{3,2,1,0:T(8,128)S(1)}, u32[]{:S(2)}, u32[]{:S(2)}) collective-permute-start(f32[4,2,32,512]{3,2,1,0:T(8,128)S(1)} %bitcast_add_fusion.11), channel_id=1, source_target_pairs={{0,32},{32,64},{64,96},{96,128},{128,160},{160,192},{192,224},{224... | collective-permute-start | bytes 1572872 | tf_op jit(solution)/shard_map/ppermute | solution.py:74
  130.3 12.4 %collective-permute-start.13 = (f32[4,2,32,512]{3,2,1,0:T(8,128)S(1)}, f32[4,2,32,512]{3,2,1,0:T(8,128)S(1)}, u32[]{:S(2)}, u32[]{:S(2)}) collective-permute-start(f32[4,2,32,512]{3,2,1,0:T(8,128)S(1)} %bitcast_add_fusion.4), channel_id=1, source_target_pairs={{0,224},{32,0},{64,32},{96,64},{128,96},{160,128},{192,160},{224,1... | collective-permute-start | bytes 1572872 | tf_op jit(solution)/shard_map/ppermute | solution.py:75
  134.1 30.7 %copy-start.3 = (f32[1,2,8,256]{3,2,1,0:T(8,128)S(1)}, f32[1,2,8,256]{3,2,1,0:T(8,128)}, u32[]{:S(2)}) copy-start(f32[1,2,8,256]{3,2,1,0:T(8,128)} %param.8) | copy-start | bytes 49156
  142.2 11.8 %collective-permute-start.4 = (f32[4,2,32,512]{3,2,1,0:T(8,128)S(1)}, f32[4,2,32,512]{3,2,1,0:T(8,128)S(1)}, u32[]{:S(2)}, u32[]{:S(2)}) collective-permute-start(f32[4,2,32,512]{3,2,1,0:T(8,128)S(1)} %bitcast_add_fusion.10), channel_id=1, source_target_pairs={{0,32},{32,64},{64,96},{96,128},{128,160},{160,192},{192,224},{224... | collective-permute-start | bytes 1572872 | tf_op jit(solution)/shard_map/ppermute | solution.py:74
  143.8 16.3 %collective-permute-start.14 = (f32[4,2,32,512]{3,2,1,0:T(8,128)S(1)}, f32[4,2,32,512]{3,2,1,0:T(8,128)S(1)}, u32[]{:S(2)}, u32[]{:S(2)}) collective-permute-start(f32[4,2,32,512]{3,2,1,0:T(8,128)S(1)} %bitcast_add_fusion.3), channel_id=1, source_target_pairs={{0,224},{32,0},{64,32},{96,64},{128,96},{160,128},{192,160},{224,1... | collective-permute-start | bytes 1572872 | tf_op jit(solution)/shard_map/ppermute | solution.py:75
  156.0 11.2 %collective-permute-start.5 = (f32[4,2,32,512]{3,2,1,0:T(8,128)}, f32[4,2,32,512]{3,2,1,0:T(8,128)}, u32[]{:S(2)}, u32[]{:S(2)}) collective-permute-start(f32[4,2,32,512]{3,2,1,0:T(8,128)} %bitcast_add_fusion.9), channel_id=1, source_target_pairs={{0,32},{32,64},{64,96},{96,128},{128,160},{160,192},{192,224},{224... | collective-permute-start | bytes 1572872 | tf_op jit(solution)/shard_map/ppermute | solution.py:74
  161.2 11.0 %collective-permute-start.15 = (f32[4,2,32,512]{3,2,1,0:T(8,128)S(1)}, f32[4,2,32,512]{3,2,1,0:T(8,128)S(1)}, u32[]{:S(2)}, u32[]{:S(2)}) collective-permute-start(f32[4,2,32,512]{3,2,1,0:T(8,128)S(1)} %bitcast_add_fusion.2), channel_id=1, source_target_pairs={{0,224},{32,0},{64,32},{96,64},{128,96},{160,128},{192,160},{224,1... | collective-permute-start | bytes 1572872 | tf_op jit(solution)/shard_map/ppermute | solution.py:75
  169.3 10.7 %collective-permute-start.6 = (f32[4,2,32,512]{3,2,1,0:T(8,128)}, f32[4,2,32,512]{3,2,1,0:T(8,128)}, u32[]{:S(2)}, u32[]{:S(2)}) collective-permute-start(f32[4,2,32,512]{3,2,1,0:T(8,128)} %bitcast_add_fusion.8), channel_id=1, source_target_pairs={{0,32},{32,64},{64,96},{96,128},{128,160},{160,192},{192,224},{224... | collective-permute-start | bytes 1572872 | tf_op jit(solution)/shard_map/ppermute | solution.py:74
  173.4 10.2 %collective-permute-start.16 = (f32[4,2,32,512]{3,2,1,0:T(8,128)S(1)}, f32[4,2,32,512]{3,2,1,0:T(8,128)S(1)}, u32[]{:S(2)}, u32[]{:S(2)}) collective-permute-start(f32[4,2,32,512]{3,2,1,0:T(8,128)S(1)} %bitcast_add_fusion.1), channel_id=1, source_target_pairs={{0,224},{32,0},{64,32},{96,64},{128,96},{160,128},{192,160},{224,1... | collective-permute-start | bytes 1572872 | tf_op jit(solution)/shard_map/ppermute | solution.py:75
  181.4 5.0 %collective-permute-start.7 = (f32[2,32,512]{2,0,1:T(2,128)S(1)}, f32[2,32,512]{2,0,1:T(2,128)S(1)}, u32[]{:S(2)}, u32[]{:S(2)}) collective-permute-start(f32[2,32,512]{2,0,1:T(2,128)S(1)} %bitcast.160), channel_id=1, source_target_pairs={{0,8},{8,16},{16,24},{24,0},{1,9},{9,17},{17,25},{25,1},{2,10},{10... | collective-permute-start | bytes 393224 | tf_op jit(solution)/shard_map/ppermute | solution.py:74
  184.8 6.3 %collective-permute-start.17 = (f32[2,32,512]{2,0,1:T(2,128)S(1)}, f32[2,32,512]{2,0,1:T(2,128)S(1)}, u32[]{:S(2)}, u32[]{:S(2)}) collective-permute-start(f32[2,32,512]{2,0,1:T(2,128)S(1)} %bitcast.161), channel_id=1, source_target_pairs={{0,24},{8,0},{16,8},{24,16},{1,25},{9,1},{17,9},{25,17},{2,26},{10... | collective-permute-start | bytes 393224 | tf_op jit(solution)/shard_map/ppermute | solution.py:75
  186.6 5.0 %collective-permute-start.8 = (f32[2,32,512]{2,0,1:T(2,128)S(1)}, f32[2,32,512]{2,0,1:T(2,128)S(1)}, u32[]{:S(2)}, u32[]{:S(2)}) collective-permute-start(f32[2,32,512]{2,0,1:T(2,128)S(1)} %bitcast_add_fusion.19), channel_id=1, source_target_pairs={{0,8},{8,16},{16,24},{24,0},{1,9},{9,17},{17,25},{25,1},{2,10},{10... | collective-permute-start | bytes 393224 | tf_op jit(solution)/shard_map/ppermute | solution.py:74
  191.2 6.3 %collective-permute-start.18 = (f32[2,32,512]{2,0,1:T(2,128)S(1)}, f32[2,32,512]{2,0,1:T(2,128)S(1)}, u32[]{:S(2)}, u32[]{:S(2)}) collective-permute-start(f32[2,32,512]{2,0,1:T(2,128)S(1)} %bitcast_add_fusion.16), channel_id=1, source_target_pairs={{0,24},{8,0},{16,8},{24,16},{1,25},{9,1},{17,9},{25,17},{2,26},{10... | collective-permute-start | bytes 393224 | tf_op jit(solution)/shard_map/ppermute | solution.py:75
  191.8 6.2 %collective-permute-start.9 = (f32[2,32,512]{2,0,1:T(2,128)S(1)}, f32[2,32,512]{2,0,1:T(2,128)S(1)}, u32[]{:S(2)}, u32[]{:S(2)}) collective-permute-start(f32[2,32,512]{2,0,1:T(2,128)S(1)} %bitcast_add_fusion.18), channel_id=1, source_target_pairs={{0,8},{8,16},{16,24},{24,0},{1,9},{9,17},{17,25},{25,1},{2,10},{10... | collective-permute-start | bytes 393224 | tf_op jit(solution)/shard_map/ppermute | solution.py:74
  197.6 6.3 %collective-permute-start.19 = (f32[2,32,512]{2,0,1:T(2,128)S(1)}, f32[2,32,512]{2,0,1:T(2,128)S(1)}, u32[]{:S(2)}, u32[]{:S(2)}) collective-permute-start(f32[2,32,512]{2,0,1:T(2,128)S(1)} %bitcast_add_fusion.15), channel_id=1, source_target_pairs={{0,24},{8,0},{16,8},{24,16},{1,25},{9,1},{17,9},{25,17},{2,26},{10... | collective-permute-start | bytes 393224 | tf_op jit(solution)/shard_map/ppermute | solution.py:75
  204.9 11.1 %all-to-all-start.2 = ((f32[2,2,32,512]{3,1,0,2:T(2,128)}), f32[2,2,32,512]{3,1,0,2:T(2,128)S(1)}, u32[]{:S(2)}, u32[]{:S(2)}) async-start(f32[2,2,32,512]{3,1,0,2:T(2,128)} %pad_maximum_fusion), calls=%async_computation.2 | async-start | bytes 524288 | tf_op jit(solution)/shard_map/all_to_all | solution.py:101
  (4 other events, 26.4 us)

commit v5 on v3

--- a/solution.py
+++ b/solution.py
@@ -87,12 +87,8 @@
     local_weights = lax.all_to_all(grouped, ("z", "x"), split_axis=0, concat_axis=0, tiled=True)
     local_weights = local_weights.reshape((zs, xs) + local_weights.shape[1:])
     mixing = mixing_matrix(local_weights, 2)
-    parts = [
-        jnp.einsum(
-            "zxpbra,rpzxat->zxpbt", mixing[:, :, o], own, preferred_element_type=jnp.float32
-        )
-        for o in range(2)
-    ]
+    both = jnp.einsum("zxopbra,rpzxat->ozxpbt", mixing, own, preferred_element_type=jnp.float32)
+    parts = [both[0], both[1]]
     parts = ring_reduce_scatter(parts, "z", zs)
     parts = ring_reduce_scatter(parts, "x", xs)
     beams = jnp.stack(parts, axis=0)

time: 203 us -> 214 us (1.054)
  local copies, waits for them, and re-layouts: 35.3 us -> 41.3 us
  waiting for transfers between devices: 77.3 us -> 79.8 us
    ppermute x10, waiting for transfers between devices: 27 us -> 41.8 us  [ring_reduce_scatter(): lax.ppermute(acc_cw, axis, forward) + pick(halves[0], position - step - 2)]
    ppermute x10, waiting for transfers between devices: 30.7 us -> 18.3 us  [ring_reduce_scatter(): lax.ppermute(acc_ccw, axis, backward) + pick(halves[1], position + step + 2)]
    slice x0 -> x1, local copies, waits for them, and re-layouts: none -> 6.92 us  [on_device(): parts = [both[0], both[1]]]
    unnamed x18 -> x12, local copies, waits for them, and re-layouts: 6.27 us -> 4.27 us
    dot_general x2 -> x1, matrix products: 6.11 us -> 8.06 us  [on_device(): jnp.einsum('zxopbra,rpzxat->ozxpbt', mixing, own, preferred_element_type=...]
  transfers between devices with their start and end apart: 23 -> 23, of which waited for: 19 -> 15; matrix products, arithmetic and copies ran while one was open for 18% -> 17% of each run, Pallas kernels for 0% -> 0%
where the time goes in v5:
time: 214 us; the launch traced here: 213 us
  waiting for transfers between devices  79.8 us (37%)
  starting transfers between devices  55 us (26%)
  local copies, waits for them, and re-layouts  41.3 us (19%)
  other arithmetic  24.6 us (11%)
  matrix products  11.9 us (6%)
    ppermute x10, waiting for transfers between devices, ring_reduce_scatter(): lax.ppermute(acc_cw, axis, forward) + pick(halves[0], position - step - 2)  41.8 us
    ppermute x10, starting transfers between devices, ring_reduce_scatter(): lax.ppermute(acc_ccw, axis, backward) + pick(halves[1], position + step + 2)  24 us
    ppermute x10, waiting for transfers between devices, ring_reduce_scatter(): lax.ppermute(acc_ccw, axis, backward) + pick(halves[1], position + step + 2)  18.3 us
    gather x2, local copies, waits for them, and re-layouts, on_device(): jnp.take(voltages, order, axis=2, mode='clip')  17.3 us
    all_to_all x1, starting transfers between devices, on_device(): lax.all_to_all(grouped, ('z', 'x'), split_axis=0, concat_axis=0, tiled=True)  11.6 us
    add x9, other arithmetic, ring_reduce_scatter(): lax.ppermute(acc_cw, axis, forward) + pick(halves[0], position - step - 2)  10.1 us
    all_to_all x1, waiting for transfers between devices, on_device(): lax.all_to_all(grouped, ('z', 'x'), split_axis=0, concat_axis=0, tiled=True)  8.82 us
    all_to_all x1, local copies, waits for them, and re-layouts, on_device(): lax.all_to_all(selected, 'c', split_axis=0, concat_axis=5, tiled=True)[0]  8.29 us
  transfers between devices with their start and end apart: 23, of which 15 were waited for; matrix products, arithmetic and copies ran while one was open for 17% of the time, Pallas kernels for 0%

profile of v5, /device:TPU:6, one launch (start us, length us, event | category | flops | bytes accessed | tf_op | source)
XLA Modules:
  0.0 213.2 jit_solution(326779204296811366)
XLA Ops:
  1.0 9.0 %gather_fusion = bf16[64,2,2,32,512]{4,3,2,1,0:T(8,128)(2,1)} fusion(bf16[2,2,64,32,512]{4,3,2,1,0:T(8,128)(2,1)} %param.5, s32[1024]{0:T(1024)S(1)} %pad_clamp_fusion), kind=kCustom, calls=%fused_computation | custom fusion | bytes 16777472 | tf_op jit(solution)/shard_map/jit(_take)/gather | solution.py:82
  10.0 8.3 %copy.31 = bf16[64,2,2,32,512]{4,3,1,2,0:T(8,128)(2,1)} copy(bf16[64,2,2,32,512]{4,3,2,1,0:T(8,128)(2,1)} %gather_fusion) | data formatting | bytes 16777216 | tf_op jit(solution)/shard_map/jit(_take)/gather | solution.py:82
  18.3 7.1 %all-to-all-start = ((bf16[2,2,2,8,4,32,512]{6,5,1,2,4,3,0:T(8,128)(2,1)}), bf16[2,2,2,8,4,32,512]{6,5,1,2,4,3,0:T(8,128)(2,1)}, u32[]{:S(2)}, u32[]{:S(2)}) async-start(bf16[2,2,2,8,4,32,512]{6,5,1,2,4,3,0:T(8,128)(2,1)} %bitcast.157), calls=%async_computation | async-start | bytes 16777216 | tf_op jit(solution)/shard_map/all_to_all | solution.py:83
  28.4 4.5 %all-to-all-done = bf16[2,2,2,8,4,32,512]{6,5,1,2,4,3,0:T(8,128)(2,1)} async-done(((bf16[2,2,2,8,4,32,512]{6,5,1,2,4,3,0:T(8,128)(2,1)}), bf16[2,2,2,8,4,32,512]{6,5,1,2,4,3,0:T(8,128)(2,1)}, u32[]{:S(2)}, u32[]{:S(2)}) %all-to-all-start) | async-done | bytes 8388640 | tf_op jit(solution)/shard_map/all_to_all | solution.py:83
  32.9 11.6 %all-to-all-start.1 = ((bf16[32,2,4096]{2,1,0:T(2,128)(2,1)}), bf16[32,2,4096]{2,1,0:T(2,128)(2,1)S(1)}, u32[]{:S(2)}, u32[]{:S(2)}) async-start(bf16[32,2,4096]{2,1,0:T(2,128)(2,1)} %reshape.84), calls=%async_computation.1 | async-start | bytes 1048576 | tf_op jit(solution)/shard_map/all_to_all | solution.py:87
  44.4 8.3 %copy.32 = bf16[1,2,2,8,4,2,32,512]{7,6,5,1,2,4,3,0:T(8,128)(2,1)} copy(bf16[1,2,2,8,4,2,32,512]{7,6,1,2,4,3,5,0:T(8,128)(2,1)} %bitcast.4) | data formatting | bytes 16777216 | tf_op jit(solution)/shard_map/all_to_all | solution.py:83
  52.7 8.8 %all-to-all-done.1 = bf16[32,2,4096]{2,1,0:T(2,128)(2,1)S(1)} async-done(((bf16[32,2,4096]{2,1,0:T(2,128)(2,1)}), bf16[32,2,4096]{2,1,0:T(2,128)(2,1)S(1)}, u32[]{:S(2)}, u32[]{:S(2)}) %all-to-all-start.1) | async-done | bytes 524320 | tf_op jit(solution)/shard_map/all_to_all | solution.py:87
  62.9 8.1 %convolution_bitcast_fusion = f32[2,8,4,2,32,512]{5,4,0,3,2,1:T(8,128)} fusion(bf16[2,2,8,4,64,512,1]{5,4,0,6,1,3,2:T(8,128)(2,1)} %bitcast.156, bf16[8,4,1,2,32,2,64]{6,4,5,2,3,1,0:T(8,128)(2,1)S(1)} %get-tuple-element.22, bf16[8,4,1,2,32,2,64]{6,4,5,2,3,1,0:T(8,128)(2,1)S(1)} %get-tuple-element.21), kind=kOutput, calls=%fused_computation.1 | convolution fusion | flops 538968064 | bytes 17825792 | tf_op jit(solution)/shard_map/zxopbra,rpzxat->ozxpbt/dot_general | solution.py:90
  71.0 6.9 %fusion.61 = (f32[1,8,4,2,32,512]{5,4,0,3,2,1:T(8,128)S(1)}, f32[1,8,4,2,32,512]{5,4,0,3,2,1:T(8,128)}) fusion(f32[2,8,4,2,32,512]{5,4,0,3,2,1:T(8,128)} %convolution_bitcast_fusion), kind=kLoop, calls=%fused_computation.119 | loop fusion | bytes 16777216 | tf_op jit(solution)/shard_map/slice | solution.py:91
  84.4 9.3 %collective-permute-done = f32[4,2,32,512]{3,2,1,0:T(8,128)S(1)} collective-permute-done((f32[4,2,32,512]{3,2,1,0:T(8,128)S(1)}, f32[4,2,32,512]{3,2,1,0:T(8,128)S(1)}, u32[]{:S(2)}, u32[]{:S(2)}) %collective-permute-start) | collective-permute-done | bytes 524320 | tf_op jit(solution)/shard_map/ppermute | solution.py:74
  96.2 3.3 %collective-permute-start.11 = (f32[4,2,32,512]{3,2,1,0:T(8,128)S(1)}, f32[4,2,32,512]{3,2,1,0:T(8,128)S(1)}, u32[]{:S(2)}, u32[]{:S(2)}) collective-permute-start(f32[4,2,32,512]{3,2,1,0:T(8,128)S(1)} %bitcast_add_fusion.6), channel_id=1, source_target_pairs={{0,224},{32,0},{64,32},{96,64},{128,96},{160,128},{192,160},{224,1... | collective-permute-start | bytes 1572872 | tf_op jit(solution)/shard_map/ppermute | solution.py:75
  99.5 8.4 %collective-permute-done.1 = f32[4,2,32,512]{3,2,1,0:T(8,128)S(1)} collective-permute-done((f32[4,2,32,512]{3,2,1,0:T(8,128)S(1)}, f32[4,2,32,512]{3,2,1,0:T(8,128)S(1)}, u32[]{:S(2)}, u32[]{:S(2)}) %collective-permute-start.1) | collective-permute-done | bytes 524320 | tf_op jit(solution)/shard_map/ppermute | solution.py:74
  113.5 7.5 %collective-permute-done.2 = f32[4,2,32,512]{3,2,1,0:T(8,128)S(1)} collective-permute-done((f32[4,2,32,512]{3,2,1,0:T(8,128)S(1)}, f32[4,2,32,512]{3,2,1,0:T(8,128)S(1)}, u32[]{:S(2)}, u32[]{:S(2)}) %collective-permute-start.2) | collective-permute-done | bytes 524320 | tf_op jit(solution)/shard_map/ppermute | solution.py:74
  123.5 3.3 %collective-permute-start.13 = (f32[4,2,32,512]{3,2,1,0:T(8,128)S(1)}, f32[4,2,32,512]{3,2,1,0:T(8,128)S(1)}, u32[]{:S(2)}, u32[]{:S(2)}) collective-permute-start(f32[4,2,32,512]{3,2,1,0:T(8,128)S(1)} %bitcast_add_fusion.4), channel_id=1, source_target_pairs={{0,224},{32,0},{64,32},{96,64},{128,96},{160,128},{192,160},{224,1... | collective-permute-start | bytes 1572872 | tf_op jit(solution)/shard_map/ppermute | solution.py:75
  126.7 6.7 %collective-permute-done.3 = f32[4,2,32,512]{3,2,1,0:T(8,128)S(1)} collective-permute-done((f32[4,2,32,512]{3,2,1,0:T(8,128)S(1)}, f32[4,2,32,512]{3,2,1,0:T(8,128)S(1)}, u32[]{:S(2)}, u32[]{:S(2)}) %collective-permute-start.3) | collective-permute-done | bytes 524320 | tf_op jit(solution)/shard_map/ppermute | solution.py:74
  139.1 5.9 %collective-permute-done.4 = f32[4,2,32,512]{3,2,1,0:T(8,128)S(1)} collective-permute-done((f32[4,2,32,512]{3,2,1,0:T(8,128)S(1)}, f32[4,2,32,512]{3,2,1,0:T(8,128)S(1)}, u32[]{:S(2)}, u32[]{:S(2)}) %collective-permute-start.4) | collective-permute-done | bytes 524320 | tf_op jit(solution)/shard_map/ppermute | solution.py:74
  147.0 4.1 %fusion.23 = (f32[512,512]{1,0:T(8,128)S(1)}, f32[512,512]{1,0:T(8,128)S(1)}) fusion(), kind=kLoop, calls=%fused_computation.52 | loop fusion | flops 3670016 | bytes 2097152 | tf_op jit(solution)/shard_map/sin | solution.py:21
  152.2 3.5 %collective-permute-start.15 = (f32[4,2,32,512]{3,2,1,0:T(8,128)S(1)}, f32[4,2,32,512]{3,2,1,0:T(8,128)S(1)}, u32[]{:S(2)}, u32[]{:S(2)}) collective-permute-start(f32[4,2,32,512]{3,2,1,0:T(8,128)S(1)} %bitcast_add_fusion.2), channel_id=1, source_target_pairs={{0,224},{32,0},{64,32},{96,64},{128,96},{160,128},{192,160},{224,1... | collective-permute-start | bytes 1572872 | tf_op jit(solution)/shard_map/ppermute | solution.py:75
  160.9 3.8 %collective-permute-done.15 = f32[4,2,32,512]{3,2,1,0:T(8,128)S(1)} collective-permute-done((f32[4,2,32,512]{3,2,1,0:T(8,128)S(1)}, f32[4,2,32,512]{3,2,1,0:T(8,128)S(1)}, u32[]{:S(2)}, u32[]{:S(2)}) %collective-permute-start.15) | collective-permute-done | bytes 524320 | tf_op jit(solution)/shard_map/ppermute | solution.py:75
  165.9 3.8 %collective-permute-start.16 = (f32[4,2,32,512]{3,2,1,0:T(8,128)S(1)}, f32[4,2,32,512]{3,2,1,0:T(8,128)S(1)}, u32[]{:S(2)}, u32[]{:S(2)}) collective-permute-start(f32[4,2,32,512]{3,2,1,0:T(8,128)S(1)} %bitcast_add_fusion.1), channel_id=1, source_target_pairs={{0,224},{32,0},{64,32},{96,64},{128,96},{160,128},{192,160},{224,1... | collective-permute-start | bytes 1572872 | tf_op jit(solution)/shard_map/ppermute | solution.py:75
  184.4 3.3 %collective-permute-start.9 = (f32[2,32,512]{2,0,1:T(2,128)S(1)}, f32[2,32,512]{2,0,1:T(2,128)S(1)}, u32[]{:S(2)}, u32[]{:S(2)}) collective-permute-start(f32[2,32,512]{2,0,1:T(2,128)S(1)} %bitcast_add_fusion.18), channel_id=1, source_target_pairs={{0,8},{8,16},{16,24},{24,0},{1,9},{9,17},{17,25},{25,1},{2,10},{10... | collective-permute-start | bytes 393224 | tf_op jit(solution)/shard_map/ppermute | solution.py:74
  190.8 6.0 %collective-permute-done.19 = f32[2,32,512]{2,0,1:T(2,128)S(1)} collective-permute-done((f32[2,32,512]{2,0,1:T(2,128)S(1)}, f32[2,32,512]{2,0,1:T(2,128)S(1)}, u32[]{:S(2)}, u32[]{:S(2)}) %collective-permute-start.19) | collective-permute-done | bytes 131104 | tf_op jit(solution)/shard_map/ppermute | solution.py:75
  197.7 4.5 %all-to-all-start.2 = ((f32[2,2,32,512]{3,1,0,2:T(2,128)}), f32[2,2,32,512]{3,1,0,2:T(2,128)S(1)}, u32[]{:S(2)}, u32[]{:S(2)}) async-start(f32[2,2,32,512]{3,1,0,2:T(2,128)} %pad_maximum_fusion), calls=%async_computation.2 | async-start | bytes 524288 | tf_op jit(solution)/shard_map/all_to_all | solution.py:96
  202.4 6.4 %all-to-all-done.2 = f32[2,2,32,512]{3,1,0,2:T(2,128)S(1)} async-done(((f32[2,2,32,512]{3,1,0,2:T(2,128)}), f32[2,2,32,512]{3,1,0,2:T(2,128)S(1)}, u32[]{:S(2)}, u32[]{:S(2)}) %all-to-all-start.2) | async-done | bytes 262176 | tf_op jit(solution)/shard_map/all_to_all | solution.py:96
  (98 shorter events, 60.3 us)
Async XLA Ops:
  18.3 14.6 %all-to-all-start = ((bf16[2,2,2,8,4,32,512]{6,5,1,2,4,3,0:T(8,128)(2,1)}), bf16[2,2,2,8,4,32,512]{6,5,1,2,4,3,0:T(8,128)(2,1)}, u32[]{:S(2)}, u32[]{:S(2)}) async-start(bf16[2,2,2,8,4,32,512]{6,5,1,2,4,3,0:T(8,128)(2,1)} %bitcast.157), calls=%async_computation | async-start | bytes 16777216 | tf_op jit(solution)/shard_map/all_to_all | solution.py:83
  32.9 28.7 %all-to-all-start.1 = ((bf16[32,2,4096]{2,1,0:T(2,128)(2,1)}), bf16[32,2,4096]{2,1,0:T(2,128)(2,1)S(1)}, u32[]{:S(2)}, u32[]{:S(2)}) async-start(bf16[32,2,4096]{2,1,0:T(2,128)(2,1)} %reshape.84), calls=%async_computation.1 | async-start | bytes 1048576 | tf_op jit(solution)/shard_map/all_to_all | solution.py:87
  79.9 13.8 %collective-permute-start = (f32[4,2,32,512]{3,2,1,0:T(8,128)S(1)}, f32[4,2,32,512]{3,2,1,0:T(8,128)S(1)}, u32[]{:S(2)}, u32[]{:S(2)}) collective-permute-start(f32[4,2,32,512]{3,2,1,0:T(8,128)S(1)} %dynamic-slice_bitcast_fusion.1), channel_id=1, source_target_pairs={{0,32},{32,64},{64,96},{96,128},{128,160},{160,192},{192,224},{224... | collective-permute-start | bytes 1572872 | tf_op jit(solution)/shard_map/ppermute | solution.py:74
  81.7 13.4 %collective-permute-start.10 = (f32[4,2,32,512]{3,2,1,0:T(8,128)S(1)}, f32[4,2,32,512]{3,2,1,0:T(8,128)S(1)}, u32[]{:S(2)}, u32[]{:S(2)}) collective-permute-start(f32[4,2,32,512]{3,2,1,0:T(8,128)S(1)} %dynamic-slice_bitcast_fusion), channel_id=1, source_target_pairs={{0,224},{32,0},{64,32},{96,64},{128,96},{160,128},{192,160},{224,1... | collective-permute-start | bytes 1572872 | tf_op jit(solution)/shard_map/ppermute | solution.py:75
  94.8 13.1 %collective-permute-start.1 = (f32[4,2,32,512]{3,2,1,0:T(8,128)S(1)}, f32[4,2,32,512]{3,2,1,0:T(8,128)S(1)}, u32[]{:S(2)}, u32[]{:S(2)}) collective-permute-start(f32[4,2,32,512]{3,2,1,0:T(8,128)S(1)} %bitcast_add_fusion.13), channel_id=1, source_target_pairs={{0,32},{32,64},{64,96},{96,128},{128,160},{160,192},{192,224},{224... | collective-permute-start | bytes 1572872 | tf_op jit(solution)/shard_map/ppermute | solution.py:74
  96.2 12.9 %collective-permute-start.11 = (f32[4,2,32,512]{3,2,1,0:T(8,128)S(1)}, f32[4,2,32,512]{3,2,1,0:T(8,128)S(1)}, u32[]{:S(2)}, u32[]{:S(2)}) collective-permute-start(f32[4,2,32,512]{3,2,1,0:T(8,128)S(1)} %bitcast_add_fusion.6), channel_id=1, source_target_pairs={{0,224},{32,0},{64,32},{96,64},{128,96},{160,128},{192,160},{224,1... | collective-permute-start | bytes 1572872 | tf_op jit(solution)/shard_map/ppermute | solution.py:75
  109.0 30.0 %copy-start.3 = (s32[8]{0:T(128)S(1)}, s32[8]{0:T(128)}, u32[]{:S(2)}) copy-start(s32[8]{0:T(128)} %param.9) | copy-start | bytes 100
  109.0 12.1 %collective-permute-start.2 = (f32[4,2,32,512]{3,2,1,0:T(8,128)S(1)}, f32[4,2,32,512]{3,2,1,0:T(8,128)S(1)}, u32[]{:S(2)}, u32[]{:S(2)}) collective-permute-start(f32[4,2,32,512]{3,2,1,0:T(8,128)S(1)} %bitcast_add_fusion.12), channel_id=1, source_target_pairs={{0,32},{32,64},{64,96},{96,128},{128,160},{160,192},{192,224},{224... | collective-permute-start | bytes 1572872 | tf_op jit(solution)/shard_map/ppermute | solution.py:74
  110.3 12.0 %collective-permute-start.12 = (f32[4,2,32,512]{3,2,1,0:T(8,128)S(1)}, f32[4,2,32,512]{3,2,1,0:T(8,128)S(1)}, u32[]{:S(2)}, u32[]{:S(2)}) collective-permute-start(f32[4,2,32,512]{3,2,1,0:T(8,128)S(1)} %bitcast_add_fusion.5), channel_id=1, source_target_pairs={{0,224},{32,0},{64,32},{96,64},{128,96},{160,128},{192,160},{224,1... | collective-permute-start | bytes 1572872 | tf_op jit(solution)/shard_map/ppermute | solution.py:75
  122.2 11.2 %collective-permute-start.3 = (f32[4,2,32,512]{3,2,1,0:T(8,128)S(1)}, f32[4,2,32,512]{3,2,1,0:T(8,128)S(1)}, u32[]{:S(2)}, u32[]{:S(2)}) collective-permute-start(f32[4,2,32,512]{3,2,1,0:T(8,128)S(1)} %bitcast_add_fusion.11), channel_id=1, source_target_pairs={{0,32},{32,64},{64,96},{96,128},{128,160},{160,192},{192,224},{224... | collective-permute-start | bytes 1572872 | tf_op jit(solution)/shard_map/ppermute | solution.py:74
  123.5 11.2 %collective-permute-start.13 = (f32[4,2,32,512]{3,2,1,0:T(8,128)S(1)}, f32[4,2,32,512]{3,2,1,0:T(8,128)S(1)}, u32[]{:S(2)}, u32[]{:S(2)}) collective-permute-start(f32[4,2,32,512]{3,2,1,0:T(8,128)S(1)} %bitcast_add_fusion.4), channel_id=1, source_target_pairs={{0,224},{32,0},{64,32},{96,64},{128,96},{160,128},{192,160},{224,1... | collective-permute-start | bytes 1572872 | tf_op jit(solution)/shard_map/ppermute | solution.py:75
  134.5 10.5 %collective-permute-start.4 = (f32[4,2,32,512]{3,2,1,0:T(8,128)S(1)}, f32[4,2,32,512]{3,2,1,0:T(8,128)S(1)}, u32[]{:S(2)}, u32[]{:S(2)}) collective-permute-start(f32[4,2,32,512]{3,2,1,0:T(8,128)S(1)} %bitcast_add_fusion.10), channel_id=1, source_target_pairs={{0,32},{32,64},{64,96},{96,128},{128,160},{160,192},{192,224},{224... | collective-permute-start | bytes 1572872 | tf_op jit(solution)/shard_map/ppermute | solution.py:74
  135.8 15.3 %collective-permute-start.14 = (f32[4,2,32,512]{3,2,1,0:T(8,128)S(1)}, f32[4,2,32,512]{3,2,1,0:T(8,128)S(1)}, u32[]{:S(2)}, u32[]{:S(2)}) collective-permute-start(f32[4,2,32,512]{3,2,1,0:T(8,128)S(1)} %bitcast_add_fusion.3), channel_id=1, source_target_pairs={{0,224},{32,0},{64,32},{96,64},{128,96},{160,128},{192,160},{224,1... | collective-permute-start | bytes 1572872 | tf_op jit(solution)/shard_map/ppermute | solution.py:75
  147.0 11.6 %collective-permute-start.5 = (f32[4,2,32,512]{3,2,1,0:T(8,128)}, f32[4,2,32,512]{3,2,1,0:T(8,128)}, u32[]{:S(2)}, u32[]{:S(2)}) collective-permute-start(f32[4,2,32,512]{3,2,1,0:T(8,128)} %bitcast_add_fusion.9), channel_id=1, source_target_pairs={{0,32},{32,64},{64,96},{96,128},{128,160},{160,192},{192,224},{224... | collective-permute-start | bytes 1572872 | tf_op jit(solution)/shard_map/ppermute | solution.py:74
  152.2 12.6 %collective-permute-start.15 = (f32[4,2,32,512]{3,2,1,0:T(8,128)S(1)}, f32[4,2,32,512]{3,2,1,0:T(8,128)S(1)}, u32[]{:S(2)}, u32[]{:S(2)}) collective-permute-start(f32[4,2,32,512]{3,2,1,0:T(8,128)S(1)} %bitcast_add_fusion.2), channel_id=1, source_target_pairs={{0,224},{32,0},{64,32},{96,64},{128,96},{160,128},{192,160},{224,1... | collective-permute-start | bytes 1572872 | tf_op jit(solution)/shard_map/ppermute | solution.py:75
  160.6 10.7 %collective-permute-start.6 = (f32[4,2,32,512]{3,2,1,0:T(8,128)}, f32[4,2,32,512]{3,2,1,0:T(8,128)}, u32[]{:S(2)}, u32[]{:S(2)}) collective-permute-start(f32[4,2,32,512]{3,2,1,0:T(8,128)} %bitcast_add_fusion.8), channel_id=1, source_target_pairs={{0,32},{32,64},{64,96},{96,128},{128,160},{160,192},{192,224},{224... | collective-permute-start | bytes 1572872 | tf_op jit(solution)/shard_map/ppermute | solution.py:74
  165.9 10.5 %collective-permute-start.16 = (f32[4,2,32,512]{3,2,1,0:T(8,128)S(1)}, f32[4,2,32,512]{3,2,1,0:T(8,128)S(1)}, u32[]{:S(2)}, u32[]{:S(2)}) collective-permute-start(f32[4,2,32,512]{3,2,1,0:T(8,128)S(1)} %bitcast_add_fusion.1), channel_id=1, source_target_pairs={{0,224},{32,0},{64,32},{96,64},{128,96},{160,128},{192,160},{224,1... | collective-permute-start | bytes 1572872 | tf_op jit(solution)/shard_map/ppermute | solution.py:75
  172.8 5.6 %collective-permute-start.7 = (f32[2,32,512]{2,0,1:T(2,128)S(1)}, f32[2,32,512]{2,0,1:T(2,128)S(1)}, u32[]{:S(2)}, u32[]{:S(2)}) collective-permute-start(f32[2,32,512]{2,0,1:T(2,128)S(1)} %bitcast.165), channel_id=1, source_target_pairs={{0,8},{8,16},{16,24},{24,0},{1,9},{9,17},{17,25},{25,1},{2,10},{10... | collective-permute-start | bytes 393224 | tf_op jit(solution)/shard_map/ppermute | solution.py:74
  177.7 6.3 %collective-permute-start.17 = (f32[2,32,512]{2,0,1:T(2,128)S(1)}, f32[2,32,512]{2,0,1:T(2,128)S(1)}, u32[]{:S(2)}, u32[]{:S(2)}) collective-permute-start(f32[2,32,512]{2,0,1:T(2,128)S(1)} %bitcast.166), channel_id=1, source_target_pairs={{0,24},{8,0},{16,8},{24,16},{1,25},{9,1},{17,9},{25,17},{2,26},{10... | collective-permute-start | bytes 393224 | tf_op jit(solution)/shard_map/ppermute | solution.py:75
  178.5 5.7 %collective-permute-start.8 = (f32[2,32,512]{2,0,1:T(2,128)S(1)}, f32[2,32,512]{2,0,1:T(2,128)S(1)}, u32[]{:S(2)}, u32[]{:S(2)}) collective-permute-start(f32[2,32,512]{2,0,1:T(2,128)S(1)} %bitcast_add_fusion.19), channel_id=1, source_target_pairs={{0,8},{8,16},{16,24},{24,0},{1,9},{9,17},{17,25},{25,1},{2,10},{10... | collective-permute-start | bytes 393224 | tf_op jit(solution)/shard_map/ppermute | solution.py:74
  184.1 6.3 %collective-permute-start.18 = (f32[2,32,512]{2,0,1:T(2,128)S(1)}, f32[2,32,512]{2,0,1:T(2,128)S(1)}, u32[]{:S(2)}, u32[]{:S(2)}) collective-permute-start(f32[2,32,512]{2,0,1:T(2,128)S(1)} %bitcast_add_fusion.16), channel_id=1, source_target_pairs={{0,24},{8,0},{16,8},{24,16},{1,25},{9,1},{17,9},{25,17},{2,26},{10... | collective-permute-start | bytes 393224 | tf_op jit(solution)/shard_map/ppermute | solution.py:75
  184.4 6.2 %collective-permute-start.9 = (f32[2,32,512]{2,0,1:T(2,128)S(1)}, f32[2,32,512]{2,0,1:T(2,128)S(1)}, u32[]{:S(2)}, u32[]{:S(2)}) collective-permute-start(f32[2,32,512]{2,0,1:T(2,128)S(1)} %bitcast_add_fusion.18), channel_id=1, source_target_pairs={{0,8},{8,16},{16,24},{24,0},{1,9},{9,17},{17,25},{25,1},{2,10},{10... | collective-permute-start | bytes 393224 | tf_op jit(solution)/shard_map/ppermute | solution.py:74
  190.5 6.3 %collective-permute-start.19 = (f32[2,32,512]{2,0,1:T(2,128)S(1)}, f32[2,32,512]{2,0,1:T(2,128)S(1)}, u32[]{:S(2)}, u32[]{:S(2)}) collective-permute-start(f32[2,32,512]{2,0,1:T(2,128)S(1)} %bitcast_add_fusion.15), channel_id=1, source_target_pairs={{0,24},{8,0},{16,8},{24,16},{1,25},{9,1},{17,9},{25,17},{2,26},{10... | collective-permute-start | bytes 393224 | tf_op jit(solution)/shard_map/ppermute | solution.py:75
  197.7 11.1 %all-to-all-start.2 = ((f32[2,2,32,512]{3,1,0,2:T(2,128)}), f32[2,2,32,512]{3,1,0,2:T(2,128)S(1)}, u32[]{:S(2)}, u32[]{:S(2)}) async-start(f32[2,2,32,512]{3,1,0,2:T(2,128)} %pad_maximum_fusion), calls=%async_computation.2 | async-start | bytes 524288 | tf_op jit(solution)/shard_map/all_to_all | solution.py:96
  (3 other events, 38.1 us)
